TPU v7x, 128 devices: a whole 4x4x4 slice. The times are simulated.
128 devices in a mesh: rows: 8 (over x, y_hi), cols: 16 (over z, y_lo, core).
Axes of the slice: x: 4, y: 4 (y_hi: 2, y_lo: 2; y = y_hi * 2 + y_lo), z: 4, core: 2. Of those that a mesh axis runs over, the one named last changes fastest.
Arguments:
- tokens: bfloat16 [256, 256, 320], P('rows', 'cols'), may hold values from -34 to 34
- norm1_gain: float32 [320], replicated, may hold values from 0.1 to 1.9
- norm1_shift: float32 [320], replicated, may hold values from -3 to 3
- w_query: bfloat16 [320, 320], replicated, may hold values from -1 to 1
- b_query: float32 [320], replicated, may hold values from -3 to 3
- w_reduce: bfloat16 [1280, 320], replicated, may hold values from -1 to 1
- b_reduce: float32 [320], replicated, may hold values from -3 to 3
- reduce_gain: float32 [320], replicated, may hold values from 0.5 to 1.5
- reduce_shift: float32 [320], replicated, may hold values from -3 to 3
- w_key: bfloat16 [320, 320], replicated, may hold values from -1 to 1
- w_value: bfloat16 [320, 320], replicated, may hold values from -0.3125 to 0.3125
- b_value: float32 [320], replicated, may hold values from -3 to 3
- w_out: bfloat16 [320, 320], replicated, may hold values from -0.75 to 0.75
- b_out: float32 [320], replicated, may hold values from -3 to 3
- norm2_gain: float32 [320], replicated, may hold values from 0.5 to 1.5
- norm2_shift: float32 [320], replicated, may hold values from -3 to 3
- w_expand: bfloat16 [320, 1280], replicated, may hold values from -0.3125 to 0.3125
- b_expand: float32 [1280], replicated, may hold values from -3 to 3
- w_depth: float32 [9, 1280], replicated, may hold values from -2 to 2
- b_depth: float32 [1280], replicated, may hold values from -3 to 3
- w_shrink: bfloat16 [1280, 320], replicated, may hold values from -0.15625 to 0.15625
- b_shrink: float32 [320], replicated, may hold values from -3 to 3
Outputs:
- block_out: bfloat16 [256, 256, 320], P('rows', 'cols')
All inputs are finite; a program needn't handle non-finite values.
Results may differ from a plain program's by a relative error of at most 0.0095.
Values may be sent and summed in bfloat16 or wider, within the bound.
No kernel may reach another device: no remote copies, remote signals or barrier semaphores. Data moves between devices by JAX's collectives and lax.ppermute only.
A program may use at most 128 MiB of HBM per device.

v0:
```python
import jax
import jax.numpy as jnp
from jax import lax
from jax.sharding import PartitionSpec as P

HEADS = 5


def padded_2(value, sides, width):
    for axis, dim in sides:
        devices, length = (lax.axis_size(axis), value.shape[dim])
        up = [(i, (i + 1) % devices) for i in range(devices - 1)]
        down = [(j, i) for i, j in up]
        last = lax.slice_in_dim(value, length - width, length, axis=dim)
        initial = lax.slice_in_dim(value, 0, width, axis=dim)
        before = lax.ppermute(last, axis, up)
        after = lax.ppermute(initial, axis, down)
        value = jnp.concatenate([before, value, after], axis=dim)
    return value


def layer_norm(value, gain, shift):
    mean = jnp.mean(value, axis=-1, keepdims=True)
    centered = value - mean
    var = jnp.mean(centered * centered, axis=-1, keepdims=True)
    return centered * lax.rsqrt(var + 1e-06) * gain + shift


def per_device(
    tokens,
    norm1_gain,
    norm1_shift,
    w_query,
    b_query,
    w_reduce,
    b_reduce,
    reduce_gain,
    reduce_shift,
    w_key,
    w_value,
    b_value,
    w_out,
    b_out,
    norm2_gain,
    norm2_shift,
    w_expand,
    b_expand,
    w_depth,
    b_depth,
    w_shrink,
    b_shrink,
):
    tile_r, tile_c, chans = tokens.shape
    head_dim = chans // HEADS
    count = tile_r * tile_c
    flat = tokens.reshape(count, chans).astype(jnp.float32)
    normed = layer_norm(flat, norm1_gain, norm1_shift).astype(jnp.bfloat16)
    query = (
        (jnp.dot(normed, w_query, preferred_element_type=jnp.float32) + b_query)
        * head_dim ** (-0.5)
    ).astype(jnp.bfloat16)
    query = query.reshape(count, HEADS, head_dim)
    blocks = (
        normed.reshape(tile_r // 2, 2, tile_c // 2, 2, chans)
        .transpose(0, 2, 1, 3, 4)
        .reshape(-1, 4 * chans)
    )
    reduced = jnp.dot(blocks, w_reduce, preferred_element_type=jnp.float32) + b_reduce
    reduced_norm = layer_norm(reduced, reduce_gain, reduce_shift).astype(jnp.bfloat16)

    def one_block(carry, keys, values):
        run_max, run_sum, accum = carry
        key_heads = keys.reshape(-1, HEADS, head_dim)
        value_heads = values.reshape(-1, HEADS, head_dim)
        scores = jnp.einsum("qhd,khd->hqk", query, key_heads, preferred_element_type=jnp.float32)
        new_max = jnp.maximum(run_max, jnp.max(scores, axis=-1))
        factor = jnp.exp(run_max - new_max)
        expo = jnp.exp(scores - new_max[..., None])
        run_sum = run_sum * factor + jnp.sum(expo, axis=-1)
        accum = accum * factor[..., None] + jnp.einsum(
            "hqk,khd->hqd",
            expo.astype(jnp.bfloat16),
            value_heads,
            preferred_element_type=jnp.float32,
        )
        return (new_max, run_sum, accum)

    start_state = (
        jnp.full((HEADS, count), -1e30, jnp.float32),
        jnp.zeros((HEADS, count), jnp.float32),
        jnp.zeros((HEADS, count, head_dim), jnp.float32),
    )
    keys = jnp.dot(reduced_norm, w_key, preferred_element_type=jnp.float32).astype(jnp.bfloat16)
    values = (jnp.dot(reduced_norm, w_value, preferred_element_type=jnp.float32) + b_value).astype(
        jnp.bfloat16
    )
    carry = start_state
    attend_keys = lax.all_gather(keys, ("rows", "cols"), axis=0, tiled=True)
    attend_values = lax.all_gather(values, ("rows", "cols"), axis=0, tiled=True)
    length = attend_keys.shape[0]

    def step(state, pair):
        return (one_block(state, pair[0], pair[1]), None)

    carry, unused = lax.scan(
        step,
        carry,
        (
            attend_keys.reshape(length // 2048, 2048, chans),
            attend_values.reshape(length // 2048, 2048, chans),
        ),
    )
    run_max, run_sum, accum = carry
    attended = (
        (accum / run_sum[..., None]).transpose(1, 0, 2).reshape(count, chans).astype(jnp.bfloat16)
    )
    mid = (flat + jnp.dot(attended, w_out, preferred_element_type=jnp.float32) + b_out).astype(
        jnp.bfloat16
    )
    normed2 = layer_norm(mid.astype(jnp.float32), norm2_gain, norm2_shift).astype(jnp.bfloat16)
    ffn = w_expand.shape[1]
    expanded = (jnp.dot(normed2, w_expand, preferred_element_type=jnp.float32) + b_expand).astype(
        jnp.bfloat16
    )
    padded = padded_2(expanded.reshape(tile_r, tile_c, ffn), (("rows", 0), ("cols", 1)), 1)
    spread = jnp.zeros((tile_r, tile_c, ffn), jnp.float32) + b_depth
    for tap_r in range(3):
        for tap_c in range(3):
            spread = (
                spread
                + padded[tap_r : tap_r + tile_r, tap_c : tap_c + tile_c, :].astype(jnp.float32)
                * w_depth[3 * tap_r + tap_c]
            )
    activated = jax.nn.gelu(spread, approximate=False).astype(jnp.bfloat16).reshape(count, ffn)
    result = (
        mid.astype(jnp.float32)
        + jnp.dot(activated, w_shrink, preferred_element_type=jnp.float32)
        + b_shrink
    )
    return result.astype(jnp.bfloat16).reshape(tile_r, tile_c, chans)


def solution(mesh):
    placed = (
        P("rows", "cols", None),
        P(),
        P(),
        P(),
        P(),
        P(),
        P(),
        P(),
        P(),
        P(),
        P(),
        P(),
        P(),
        P(),
        P(),
        P(),
        P(),
        P(),
        P(),
        P(),
        P(),
        P(),
    )
    return jax.shard_map(
        per_device, mesh=mesh, in_specs=placed, out_specs=P("rows", "cols", None), check_vma=False
    )
```

profile of v0, /device:TPU:15, one launch (start us, length us, event | category | flops | bytes accessed | tf_op | source)
XLA Modules:
  0.0 747.8 jit_solution(7699184805507884960)
XLA Ops:
  6.6 1.5 reshape.158
  8.1 1.1 convert_reduce_fusion
  9.3 1.3 multiply_reduce_fusion
  10.9 0.3 copy.53
  11.1 0.3 copy.50
  11.4 0.2 fusion.33
  11.6 0.3 copy.54
  11.9 0.3 reshape.150
  12.3 0.4 fusion.42
  12.8 1.0 convolution_convert_fusion
  13.9 1.0 fusion.28
  15.2 1.1 copy.57
  16.4 1.5 fusion.24
  17.8 222.8 %all-gather.3.cloned.1.call-done = bf16[16384,320]{0,1:T(8,128)(2,1)} async-done(((bf16[128,320]{0,1:T(8,128)(2,1)}), bf16[16384,320]{0,1:T(8,128)(2,1)}) %all-gather.3.cloned.1.call-update) | async-done | bytes 10485776 | tf_op jit(solution)/shard_map/all_gather | solution.py:98
  240.7 10.1 %copy.80 = bf16[40,8,8,2048]{3,2,0,1:T(8,128)(2,1)} copy(bf16[40,8,8,2048]{3,2,1,0:T(8,128)(2,1)} %bitcast.73) | data formatting | bytes 20971520 | tf_op jit(solution)/shard_map/reshape | solution.py:109
  250.8 215.9 %all-gather.5.cloned.1.call-done = bf16[16384,320]{0,1:T(8,128)(2,1)} async-done(((bf16[128,320]{0,1:T(8,128)(2,1)}), bf16[16384,320]{0,1:T(8,128)(2,1)}) %all-gather.5.cloned.1.call-update) | async-done | bytes 10485776 | tf_op jit(solution)/shard_map/all_gather | solution.py:99
  466.7 10.0 %copy.79 = bf16[40,8,8,2048]{3,2,0,1:T(8,128)(2,1)} copy(bf16[40,8,8,2048]{3,2,1,0:T(8,128)(2,1)} %bitcast.74) | data formatting | bytes 20971520 | tf_op jit(solution)/shard_map/reshape | solution.py:110
  476.7 225.4 %while.15 = (s32[]{:T(128)}, f32[5,512]{1,0:T(8,128)S(1)}, f32[5,512]{1,0:T(8,128)S(1)}, f32[5,512,64]{1,2,0:T(8,128)S(1)}, bf16[8,2048,320]{1,2,0:T(8,128)(2,1)...) while((s32[]{:T(128)}, f32[5,512]{1,0:T(8,128)S(1)}, ...), condition=%wide.region_7.8_spmd.clone, body=%wide.region_4.7_spmd.clone.sunk | while | flops 1368896000 | bytes 72581232 | solution.py:105
  476.7 2.0 constant_dynamic-slice_fusion.3
  478.7 8.6 %bitcast_reduce_fusion.2 = (f32[5,512]{1,0:T(8,128)S(1)}, f32[5,2048,512]{2,1,0:T(8,128)}) fusion(bf16[2048,5,64]{0,2,1:T(8,128)(2,1)S(1)} %bitcast.65, bf16[512,5,64]{0,2,1:T(8,128)(2,1)S(1)} %get-tuple-element.214), kind=kOutput, calls=%fused_computation.1.clone.1 | convolution fusion | flops 676328960 | bytes 22620160 | tf_op jit(solution)/shard_map/while/body/eval_jaxpr/qhd,khd->hqk/dot_general | solution.py:75
  487.4 8.8 %fusion.68 = f32[5,512]{1,0:T(8,128)S(1)} fusion(f32[5,2048,512]{2,1,0:T(8,128)} %get-tuple-element.187, f32[5,512]{1,0:T(8,128)S(1)} %select_maximum_fusion.2), kind=kLoop, calls=%fused_computation.4.clone.1 | loop fusion | flops 10483200 | bytes 20992000 | tf_op jit(solution)/shard_map/while/body/eval_jaxpr/reduce_sum | solution.py:79
  496.2 8.7 %fusion.70 = f32[5,512,64]{1,2,0:T(8,128)S(1)} fusion(bf16[2048,5,64]{0,2,1:T(8,128)(2,1)S(1)} %bitcast.66, f32[5,2048,512]{2,1,0:T(8,128)} %get-tuple-element.187, f32[5,512]{1,0:T(8,128)S(1)} %select_maximum_fusion.2, f32[5,512,64]{1,2,0:T(8,128)S(1)} %get-tuple-element.203, f32[5,512]{1,0:T(8,128)S(1)} %get-tuple-element.190, pred[]{:T(512)S(6)} %compare.3), kind=kOutput, calls=%fused_computation.7.clone.1 | convolution fusion | flops 682065920 | bytes 23613440 | tf_op jit(solution)/shard_map/while/body/eval_jaxpr/hqk,khd->hqd/dot_general | solution.py:80
  504.9 2.0 constant_dynamic-slice_fusion.3
  506.9 8.6 %bitcast_reduce_fusion.2 = (f32[5,512]{1,0:T(8,128)S(1)}, f32[5,2048,512]{2,1,0:T(8,128)}) fusion(bf16[2048,5,64]{0,2,1:T(8,128)(2,1)S(1)} %bitcast.65, bf16[512,5,64]{0,2,1:T(8,128)(2,1)S(1)} %get-tuple-element.214), kind=kOutput, calls=%fused_computation.1.clone.1 | convolution fusion | flops 676328960 | bytes 22620160 | tf_op jit(solution)/shard_map/while/body/eval_jaxpr/qhd,khd->hqk/dot_general | solution.py:75
  515.5 8.8 %fusion.68 = f32[5,512]{1,0:T(8,128)S(1)} fusion(f32[5,2048,512]{2,1,0:T(8,128)} %get-tuple-element.187, f32[5,512]{1,0:T(8,128)S(1)} %select_maximum_fusion.2), kind=kLoop, calls=%fused_computation.4.clone.1 | loop fusion | flops 10483200 | bytes 20992000 | tf_op jit(solution)/shard_map/while/body/eval_jaxpr/reduce_sum | solution.py:79
  524.3 8.7 %fusion.70 = f32[5,512,64]{1,2,0:T(8,128)S(1)} fusion(bf16[2048,5,64]{0,2,1:T(8,128)(2,1)S(1)} %bitcast.66, f32[5,2048,512]{2,1,0:T(8,128)} %get-tuple-element.187, f32[5,512]{1,0:T(8,128)S(1)} %select_maximum_fusion.2, f32[5,512,64]{1,2,0:T(8,128)S(1)} %get-tuple-element.203, f32[5,512]{1,0:T(8,128)S(1)} %get-tuple-element.190, pred[]{:T(512)S(6)} %compare.3), kind=kOutput, calls=%fused_computation.7.clone.1 | convolution fusion | flops 682065920 | bytes 23613440 | tf_op jit(solution)/shard_map/while/body/eval_jaxpr/hqk,khd->hqd/dot_general | solution.py:80
  533.1 2.0 constant_dynamic-slice_fusion.3
  535.1 8.6 %bitcast_reduce_fusion.2 = (f32[5,512]{1,0:T(8,128)S(1)}, f32[5,2048,512]{2,1,0:T(8,128)}) fusion(bf16[2048,5,64]{0,2,1:T(8,128)(2,1)S(1)} %bitcast.65, bf16[512,5,64]{0,2,1:T(8,128)(2,1)S(1)} %get-tuple-element.214), kind=kOutput, calls=%fused_computation.1.clone.1 | convolution fusion | flops 676328960 | bytes 22620160 | tf_op jit(solution)/shard_map/while/body/eval_jaxpr/qhd,khd->hqk/dot_general | solution.py:75
  543.7 8.8 %fusion.68 = f32[5,512]{1,0:T(8,128)S(1)} fusion(f32[5,2048,512]{2,1,0:T(8,128)} %get-tuple-element.187, f32[5,512]{1,0:T(8,128)S(1)} %select_maximum_fusion.2), kind=kLoop, calls=%fused_computation.4.clone.1 | loop fusion | flops 10483200 | bytes 20992000 | tf_op jit(solution)/shard_map/while/body/eval_jaxpr/reduce_sum | solution.py:79
  552.5 8.7 %fusion.70 = f32[5,512,64]{1,2,0:T(8,128)S(1)} fusion(bf16[2048,5,64]{0,2,1:T(8,128)(2,1)S(1)} %bitcast.66, f32[5,2048,512]{2,1,0:T(8,128)} %get-tuple-element.187, f32[5,512]{1,0:T(8,128)S(1)} %select_maximum_fusion.2, f32[5,512,64]{1,2,0:T(8,128)S(1)} %get-tuple-element.203, f32[5,512]{1,0:T(8,128)S(1)} %get-tuple-element.190, pred[]{:T(512)S(6)} %compare.3), kind=kOutput, calls=%fused_computation.7.clone.1 | convolution fusion | flops 682065920 | bytes 23613440 | tf_op jit(solution)/shard_map/while/body/eval_jaxpr/hqk,khd->hqd/dot_general | solution.py:80
  561.3 2.0 constant_dynamic-slice_fusion.3
  563.2 8.6 %bitcast_reduce_fusion.2 = (f32[5,512]{1,0:T(8,128)S(1)}, f32[5,2048,512]{2,1,0:T(8,128)}) fusion(bf16[2048,5,64]{0,2,1:T(8,128)(2,1)S(1)} %bitcast.65, bf16[512,5,64]{0,2,1:T(8,128)(2,1)S(1)} %get-tuple-element.214), kind=kOutput, calls=%fused_computation.1.clone.1 | convolution fusion | flops 676328960 | bytes 22620160 | tf_op jit(solution)/shard_map/while/body/eval_jaxpr/qhd,khd->hqk/dot_general | solution.py:75
  571.9 8.8 %fusion.68 = f32[5,512]{1,0:T(8,128)S(1)} fusion(f32[5,2048,512]{2,1,0:T(8,128)} %get-tuple-element.187, f32[5,512]{1,0:T(8,128)S(1)} %select_maximum_fusion.2), kind=kLoop, calls=%fused_computation.4.clone.1 | loop fusion | flops 10483200 | bytes 20992000 | tf_op jit(solution)/shard_map/while/body/eval_jaxpr/reduce_sum | solution.py:79
  580.7 8.7 %fusion.70 = f32[5,512,64]{1,2,0:T(8,128)S(1)} fusion(bf16[2048,5,64]{0,2,1:T(8,128)(2,1)S(1)} %bitcast.66, f32[5,2048,512]{2,1,0:T(8,128)} %get-tuple-element.187, f32[5,512]{1,0:T(8,128)S(1)} %select_maximum_fusion.2, f32[5,512,64]{1,2,0:T(8,128)S(1)} %get-tuple-element.203, f32[5,512]{1,0:T(8,128)S(1)} %get-tuple-element.190, pred[]{:T(512)S(6)} %compare.3), kind=kOutput, calls=%fused_computation.7.clone.1 | convolution fusion | flops 682065920 | bytes 23613440 | tf_op jit(solution)/shard_map/while/body/eval_jaxpr/hqk,khd->hqd/dot_general | solution.py:80
  589.4 2.0 constant_dynamic-slice_fusion.3
  591.4 8.6 %bitcast_reduce_fusion.2 = (f32[5,512]{1,0:T(8,128)S(1)}, f32[5,2048,512]{2,1,0:T(8,128)}) fusion(bf16[2048,5,64]{0,2,1:T(8,128)(2,1)S(1)} %bitcast.65, bf16[512,5,64]{0,2,1:T(8,128)(2,1)S(1)} %get-tuple-element.214), kind=kOutput, calls=%fused_computation.1.clone.1 | convolution fusion | flops 676328960 | bytes 22620160 | tf_op jit(solution)/shard_map/while/body/eval_jaxpr/qhd,khd->hqk/dot_general | solution.py:75
  600.0 8.8 %fusion.68 = f32[5,512]{1,0:T(8,128)S(1)} fusion(f32[5,2048,512]{2,1,0:T(8,128)} %get-tuple-element.187, f32[5,512]{1,0:T(8,128)S(1)} %select_maximum_fusion.2), kind=kLoop, calls=%fused_computation.4.clone.1 | loop fusion | flops 10483200 | bytes 20992000 | tf_op jit(solution)/shard_map/while/body/eval_jaxpr/reduce_sum | solution.py:79
  608.8 8.7 %fusion.70 = f32[5,512,64]{1,2,0:T(8,128)S(1)} fusion(bf16[2048,5,64]{0,2,1:T(8,128)(2,1)S(1)} %bitcast.66, f32[5,2048,512]{2,1,0:T(8,128)} %get-tuple-element.187, f32[5,512]{1,0:T(8,128)S(1)} %select_maximum_fusion.2, f32[5,512,64]{1,2,0:T(8,128)S(1)} %get-tuple-element.203, f32[5,512]{1,0:T(8,128)S(1)} %get-tuple-element.190, pred[]{:T(512)S(6)} %compare.3), kind=kOutput, calls=%fused_computation.7.clone.1 | convolution fusion | flops 682065920 | bytes 23613440 | tf_op jit(solution)/shard_map/while/body/eval_jaxpr/hqk,khd->hqd/dot_general | solution.py:80
  617.6 2.0 constant_dynamic-slice_fusion.3
  619.6 8.6 %bitcast_reduce_fusion.2 = (f32[5,512]{1,0:T(8,128)S(1)}, f32[5,2048,512]{2,1,0:T(8,128)}) fusion(bf16[2048,5,64]{0,2,1:T(8,128)(2,1)S(1)} %bitcast.65, bf16[512,5,64]{0,2,1:T(8,128)(2,1)S(1)} %get-tuple-element.214), kind=kOutput, calls=%fused_computation.1.clone.1 | convolution fusion | flops 676328960 | bytes 22620160 | tf_op jit(solution)/shard_map/while/body/eval_jaxpr/qhd,khd->hqk/dot_general | solution.py:75
  628.2 8.8 %fusion.68 = f32[5,512]{1,0:T(8,128)S(1)} fusion(f32[5,2048,512]{2,1,0:T(8,128)} %get-tuple-element.187, f32[5,512]{1,0:T(8,128)S(1)} %select_maximum_fusion.2), kind=kLoop, calls=%fused_computation.4.clone.1 | loop fusion | flops 10483200 | bytes 20992000 | tf_op jit(solution)/shard_map/while/body/eval_jaxpr/reduce_sum | solution.py:79
  637.0 8.7 %fusion.70 = f32[5,512,64]{1,2,0:T(8,128)S(1)} fusion(bf16[2048,5,64]{0,2,1:T(8,128)(2,1)S(1)} %bitcast.66, f32[5,2048,512]{2,1,0:T(8,128)} %get-tuple-element.187, f32[5,512]{1,0:T(8,128)S(1)} %select_maximum_fusion.2, f32[5,512,64]{1,2,0:T(8,128)S(1)} %get-tuple-element.203, f32[5,512]{1,0:T(8,128)S(1)} %get-tuple-element.190, pred[]{:T(512)S(6)} %compare.3), kind=kOutput, calls=%fused_computation.7.clone.1 | convolution fusion | flops 682065920 | bytes 23613440 | tf_op jit(solution)/shard_map/while/body/eval_jaxpr/hqk,khd->hqd/dot_general | solution.py:80
  645.8 2.0 constant_dynamic-slice_fusion.3
  647.7 8.6 %bitcast_reduce_fusion.2 = (f32[5,512]{1,0:T(8,128)S(1)}, f32[5,2048,512]{2,1,0:T(8,128)}) fusion(bf16[2048,5,64]{0,2,1:T(8,128)(2,1)S(1)} %bitcast.65, bf16[512,5,64]{0,2,1:T(8,128)(2,1)S(1)} %get-tuple-element.214), kind=kOutput, calls=%fused_computation.1.clone.1 | convolution fusion | flops 676328960 | bytes 22620160 | tf_op jit(solution)/shard_map/while/body/eval_jaxpr/qhd,khd->hqk/dot_general | solution.py:75
  656.4 8.8 %fusion.68 = f32[5,512]{1,0:T(8,128)S(1)} fusion(f32[5,2048,512]{2,1,0:T(8,128)} %get-tuple-element.187, f32[5,512]{1,0:T(8,128)S(1)} %select_maximum_fusion.2), kind=kLoop, calls=%fused_computation.4.clone.1 | loop fusion | flops 10483200 | bytes 20992000 | tf_op jit(solution)/shard_map/while/body/eval_jaxpr/reduce_sum | solution.py:79
  665.2 8.7 %fusion.70 = f32[5,512,64]{1,2,0:T(8,128)S(1)} fusion(bf16[2048,5,64]{0,2,1:T(8,128)(2,1)S(1)} %bitcast.66, f32[5,2048,512]{2,1,0:T(8,128)} %get-tuple-element.187, f32[5,512]{1,0:T(8,128)S(1)} %select_maximum_fusion.2, f32[5,512,64]{1,2,0:T(8,128)S(1)} %get-tuple-element.203, f32[5,512]{1,0:T(8,128)S(1)} %get-tuple-element.190, pred[]{:T(512)S(6)} %compare.3), kind=kOutput, calls=%fused_computation.7.clone.1 | convolution fusion | flops 682065920 | bytes 23613440 | tf_op jit(solution)/shard_map/while/body/eval_jaxpr/hqk,khd->hqd/dot_general | solution.py:80
  673.9 2.0 constant_dynamic-slice_fusion.3
  675.9 8.6 %bitcast_reduce_fusion.2 = (f32[5,512]{1,0:T(8,128)S(1)}, f32[5,2048,512]{2,1,0:T(8,128)}) fusion(bf16[2048,5,64]{0,2,1:T(8,128)(2,1)S(1)} %bitcast.65, bf16[512,5,64]{0,2,1:T(8,128)(2,1)S(1)} %get-tuple-element.214), kind=kOutput, calls=%fused_computation.1.clone.1 | convolution fusion | flops 676328960 | bytes 22620160 | tf_op jit(solution)/shard_map/while/body/eval_jaxpr/qhd,khd->hqk/dot_general | solution.py:75
  684.5 8.8 %fusion.68 = f32[5,512]{1,0:T(8,128)S(1)} fusion(f32[5,2048,512]{2,1,0:T(8,128)} %get-tuple-element.187, f32[5,512]{1,0:T(8,128)S(1)} %select_maximum_fusion.2), kind=kLoop, calls=%fused_computation.4.clone.1 | loop fusion | flops 10483200 | bytes 20992000 | tf_op jit(solution)/shard_map/while/body/eval_jaxpr/reduce_sum | solution.py:79
  693.4 8.7 %fusion.70 = f32[5,512,64]{1,2,0:T(8,128)S(1)} fusion(bf16[2048,5,64]{0,2,1:T(8,128)(2,1)S(1)} %bitcast.66, f32[5,2048,512]{2,1,0:T(8,128)} %get-tuple-element.187, f32[5,512]{1,0:T(8,128)S(1)} %select_maximum_fusion.2, f32[5,512,64]{1,2,0:T(8,128)S(1)} %get-tuple-element.203, f32[5,512]{1,0:T(8,128)S(1)} %get-tuple-element.190, pred[]{:T(512)S(6)} %compare.3), kind=kOutput, calls=%fused_computation.7.clone.1 | convolution fusion | flops 682065920 | bytes 23613440 | tf_op jit(solution)/shard_map/while/body/eval_jaxpr/hqk,khd->hqd/dot_general | solution.py:80
  702.2 1.5 fusion.43
  703.9 1.0 fusion.10
  704.9 3.7 collective-permute-start.1
  708.6 3.3 collective-permute-start
  711.9 3.8 collective-permute-done
  715.8 0.3 pad_maximum_fusion.5
  716.0 5.4 collective-permute-start.2
  721.4 1.9 collective-permute-start.3
  723.5 0.3 collective-permute-done.2
  723.8 5.3 collective-permute-done.3
  729.1 1.3 maximum_maximum_fusion
  730.4 9.0 %fusion.13 = bf16[32,16,1280]{2,1,0:T(8,128)(2,1)S(1)} fusion(bf16[32,16,1280]{2,1,0:T(8,128)(2,1)S(1)} %bitcast.72, bf16[34,17,1280]{2,1,0:T(8,128)(2,1)S(1)} %get-tuple-element.127, bf16[1,16,1280]{2,1,0:T(8,128)(2,1)S(1)} %collective-permute-done.1, bf16[34,17,1280]{2,1,0:T(8,128)(2,1)S(1)} %get-tuple-element.126, ...), kind=kLoop, calls=%fused_computation.22 | loop fusion | flops 61603840 | bytes 10618880 | tf_op jit(solution)/shard_map/convert_element_type | solution.py:134
  739.4 0.6 fusion.27
  740.0 0.9 copy.58
  (90 shorter events, 1.2 us)
Async XLA Ops:
  6.5 697.3 %copy-start = (bf16[320,1280]{1,0:T(8,128)(2,1)S(1)}, bf16[320,1280]{1,0:T(8,128)(2,1)}, u32[]{:S(2)}) copy-start(bf16[320,1280]{1,0:T(8,128)(2,1)} %param.40) | copy-start | bytes 2457604
  6.5 4.8 copy-start.12
  6.5 4.9 copy-start.13
  6.5 5.7 copy-start.10
  6.5 5.7 copy-start.2
  6.5 234.1 %all-gather.3.cloned.1.call-start = ((), (), s32[]{:S(2)}) async-start(), calls=%async_computation | async-start | bytes 10567680 | tf_op jit(solution)/shard_map/all_gather | solution.py:98
  9.3 3.5 copy-start.4
  9.3 3.5 copy-start.7
  9.3 3.5 copy-start.8
  10.7 3.2 copy-start.5
  10.8 3.2 copy-start.11
  11.4 3.6 copy-start.1
  12.3 4.1 copy-start.17
  13.9 452.9 %all-gather.5.cloned.1.call-start = ((), (), s32[]{:S(2)}) async-start(), calls=%async_computation.1 | async-start | bytes 10567680 | tf_op jit(solution)/shard_map/all_gather | solution.py:99
  476.7 225.5 %copy-start.3 = (bf16[320,320]{1,0:T(8,128)(2,1)S(1)}, bf16[320,320]{1,0:T(8,128)(2,1)}, u32[]{:S(2)}) copy-start(bf16[320,320]{1,0:T(8,128)(2,1)} %param.36) | copy-start | bytes 614404
  476.7 225.5 %copy-start.14 = (f32[320]{0:T(512)S(1)}, f32[320]{0:T(512)}, u32[]{:S(2)}) copy-start(f32[320]{0:T(512)} %param.37) | copy-start | bytes 3844
  702.1 1.8 copy-start.16
  702.1 1.8 copy-start.18
  702.1 1.8 copy-start.19
  703.9 19.5 %copy-start.6 = (f32[9,1280]{1,0:T(8,128)S(1)}, f32[9,1280]{1,0:T(8,128)}, u32[]{:S(2)}) copy-start(f32[9,1280]{1,0:T(8,128)} %param.42) | copy-start | bytes 138244
  704.9 7.0 collective-permute-start.1
  708.6 7.1 collective-permute-start
  716.0 7.7 %collective-permute-start.2 = (bf16[34,1,1280]{2,1,0:T(2,128)(2,1)S(1)}, bf16[34,1,1280]{2,1,0:T(2,128)(2,1)S(1)}, u32[]{:S(2)}, u32[]{:S(2)}) collective-permute-start(bf16[34,1,1280]{2,1,0:T(2,128)(2,1)S(1)} %get-tuple-element.128), channel_id=1, source_target_pairs={{0,1},{1,2},{2,3},{3,4},{4,5},{5,6},{6,7},{7,8},{8,9},{9,10},{10,1... | collective-permute-start | bytes 261128 | tf_op jit(solution)/shard_map/ppermute | solution.py:16
  721.4 7.6 %collective-permute-start.3 = (bf16[34,1,1280]{2,1,0:T(2,128)(2,1)S(1)}, bf16[34,1,1280]{2,1,0:T(2,128)(2,1)S(1)}, u32[]{:S(2)}, u32[]{:S(2)}) collective-permute-start(bf16[34,1,1280]{2,1,0:T(2,128)(2,1)S(1)} %get-tuple-element.129), channel_id=1, source_target_pairs={{1,0},{2,1},{3,2},{4,3},{5,4},{6,5},{7,6},{8,7},{9,8},{10,9},{11,1... | collective-permute-start | bytes 261128 | tf_op jit(solution)/shard_map/ppermute | solution.py:17
  723.5 6.8 copy-start.9
  730.3 9.0 %copy-start.15 = (bf16[1280,320]{0,1:T(8,128)(2,1)S(1)}, bf16[1280,320]{0,1:T(8,128)(2,1)}, u32[]{:S(2)}) copy-start(bf16[1280,320]{0,1:T(8,128)(2,1)} %param.44) | copy-start | bytes 2457604
  730.4 9.0 %copy-start.20 = (f32[320]{0:T(512)S(1)}, f32[320]{0:T(512)}, u32[]{:S(2)}) copy-start(f32[320]{0:T(512)} %param.45) | copy-start | bytes 3844
Sparse Core Ops, SparseCore 0:
  14.0 226.6 all-gather.2
  242.3 224.3 all-gather.4
where the time goes:
time: 749 us; the launch traced here: 748 us
  waiting for transfers between devices  448 us (60%)
  matrix products  146 us (19%)
  other arithmetic  84 us (11%)
  local copies, waits for them, and re-layouts  41.2 us (6%)
  starting transfers between devices  14.3 us (2%)
  between operations  13.9 us (2%)
    all_gather x1, waiting for transfers between devices, per_device(): attend_keys = lax.all_gather(keys, ('rows', 'cols'), axis=0, tiled=True)  223 us
    all_gather x1, waiting for transfers between devices, per_device(): attend_values = lax.all_gather(values, ('rows', 'cols'), axis=0, tiled=True)  216 us
    reduce_sum x8, other arithmetic, one_block(): run_sum = run_sum * factor + jnp.sum(expo, axis=-1)  70.3 us
    dot_general x8, matrix products, one_block(): jnp.einsum('hqk,khd->hqd', expo.astype(jnp.bfloat16), value_heads, prefer...  69.8 us
    dot_general x8, matrix products, one_block(): jnp.einsum('qhd,khd->hqk', query, key_heads, preferred_element_type=jnp.f...  69 us
    dynamic_slice x8, local copies, waits for them, and re-layouts, per_device(): lax.scan(step, carry, (attend_keys.reshape(length // 2048, 2048, chans),...  15.7 us
  transfers between devices with their start and end apart: 6, of which 5 were waited for; matrix products, arithmetic and copies ran while one was open for 2% of the time, Pallas kernels for 0%

commit v1 on v0

--- a/solution.py
+++ b/solution.py
@@ -90,13 +90,13 @@
         jnp.zeros((HEADS, count), jnp.float32),
         jnp.zeros((HEADS, count, head_dim), jnp.float32),
     )
-    keys = jnp.dot(reduced_norm, w_key, preferred_element_type=jnp.float32).astype(jnp.bfloat16)
-    values = (jnp.dot(reduced_norm, w_value, preferred_element_type=jnp.float32) + b_value).astype(
-        jnp.bfloat16
-    )
+    gathered = lax.all_gather(reduced_norm, "rows", axis=0, tiled=True)
+    gathered = lax.all_gather(gathered, "cols", axis=0, tiled=True)
+    attend_keys = jnp.dot(gathered, w_key, preferred_element_type=jnp.float32).astype(jnp.bfloat16)
+    attend_values = (
+        jnp.dot(gathered, w_value, preferred_element_type=jnp.float32) + b_value
+    ).astype(jnp.bfloat16)
     carry = start_state
-    attend_keys = lax.all_gather(keys, ("rows", "cols"), axis=0, tiled=True)
-    attend_values = lax.all_gather(values, ("rows", "cols"), axis=0, tiled=True)
     length = attend_keys.shape[0]
 
     def step(state, pair):

time: 749 us -> 414 us (0.55)
  waiting for transfers between devices: 448 us -> 77.2 us
  blocking collectives: 0 us -> 28.3 us
  matrix products: 146 us -> 162 us
  local copies, waits for them, and re-layouts: 41.2 us -> 33.1 us
    all_gather x2 -> x1, waiting for transfers between devices: 439 us -> 67.3 us  [per_device(): gathered = lax.all_gather(gathered, 'cols', axis=0, tiled=True)]
    all_gather x0 -> x1, blocking collectives: none -> 28.3 us  [per_device(): gathered = lax.all_gather(reduced_norm, 'rows', axis=0, tiled=True)]
    reshape x2 -> x0, local copies, waits for them, and re-layouts: 20.1 us -> none  [the longest x1 10.1 us: per_device(): attend_keys.reshape(length // 2048, 2048, chans)]
    dot_general x2, matrix products: 2.06 us -> 19 us  [the longest x1 10.7 us: per_device(): jnp.dot(gathered, w_value, preferred_element_type=jnp.float32) + b_value]
    unnamed x42 -> x45, local copies, waits for them, and re-layouts: 0.11 us -> 12.2 us
  transfers between devices with their start and end apart: 6 -> 5, of which waited for: 5 -> 4; matrix products, arithmetic and copies ran while one was open for 2% -> 0% of each run, Pallas kernels for 0% -> 0%
where the time goes in v1:
time: 414 us; the launch traced here: 413 us
  matrix products  162 us (39%)
  other arithmetic  84.1 us (20%)
  waiting for transfers between devices  77.2 us (19%)
  local copies, waits for them, and re-layouts  33.1 us (8%)
  blocking collectives  28.3 us (7%)
  starting transfers between devices  14.5 us (4%)
  between operations  13.9 us (3%)
    reduce_sum x8, other arithmetic, one_block(): run_sum = run_sum * factor + jnp.sum(expo, axis=-1)  70.3 us
    dot_general x8, matrix products, one_block(): jnp.einsum('hqk,khd->hqd', expo.astype(jnp.bfloat16), value_heads, prefer...  69.8 us
    dot_general x8, matrix products, one_block(): jnp.einsum('qhd,khd->hqk', query, key_heads, preferred_element_type=jnp.f...  69 us
    all_gather x1, waiting for transfers between devices, per_device(): gathered = lax.all_gather(gathered, 'cols', axis=0, tiled=True)  67.3 us
    all_gather x1, blocking collectives, per_device(): gathered = lax.all_gather(reduced_norm, 'rows', axis=0, tiled=True)  28.3 us
    dynamic_slice x8, local copies, waits for them, and re-layouts, per_device(): lax.scan(step, carry, (attend_keys.reshape(length // 2048, 2048, chans),...  15.7 us
    unnamed x45, local copies, waits for them, and re-layouts  12.2 us
    dot_general x1, matrix products, per_device(): jnp.dot(gathered, w_value, preferred_element_type=jnp.float32) + b_value  10.7 us
  transfers between devices with their start and end apart: 5, of which 4 were waited for; matrix products, arithmetic and copies ran while one was open for 0% of the time, Pallas kernels for 0%

profile of v1, /device:TPU:15, one launch (start us, length us, event | category | flops | bytes accessed | tf_op | source)
XLA Modules:
  0.0 413.4 jit_solution(11138008329299714225)
XLA Ops:
  6.6 1.5 reshape.158
  8.1 1.1 convert_reduce_fusion
  9.3 1.3 multiply_reduce_fusion
  10.8 0.3 copy.53
  11.0 0.3 copy.50
  11.3 0.2 fusion.33
  11.6 0.3 copy.54
  11.9 0.3 reshape.150
  12.2 0.4 fusion.42
  12.7 0.2 add_convert_fusion.4
  12.9 28.3 %all_gather.6 = bf16[1024,320]{0,1:T(8,128)(2,1)} all-gather(bf16[128,320]{0,1:T(8,128)(2,1)S(1)} %add_convert_fusion.4), channel_id=1, replica_groups=mesh['rows'=8,'cols'=16] {'rows'}, dimensions={0}, use_global_device_ids=true | all-gather | bytes 737280 | tf_op jit(solution)/shard_map/all_gather | solution.py:93
  41.5 1.1 copy.57
  42.6 0.5 fusion.25
  43.2 67.3 %all-gather.2.cloned.1.call-done = bf16[16384,320]{0,1:T(8,128)(2,1)} async-done(((bf16[1024,320]{0,1:T(8,128)(2,1)}), bf16[16384,320]{0,1:T(8,128)(2,1)}) %all-gather.2.cloned.1.call-update) | async-done | bytes 10485776 | tf_op jit(solution)/shard_map/all_gather | solution.py:94
  110.5 8.4 %convolution_convert_fusion = bf16[16384,320]{0,1:T(8,128)(2,1)S(1)} fusion(bf16[16384,320]{0,1:T(8,128)(2,1)} %all-gather.2.cloned.1.call-done, bf16[320,320]{1,0:T(8,128)(2,1)S(1)} %copy-done.4), kind=kOutput, calls=%fused_computation.17 | convolution fusion | flops 3360686080 | bytes 21176320 | tf_op jit(solution)/shard_map/dot_general | solution.py:95
  118.8 10.7 %fusion.10 = bf16[16384,320]{0,1:T(8,128)(2,1)} fusion(bf16[16384,320]{0,1:T(8,128)(2,1)} %all-gather.2.cloned.1.call-done, bf16[320,320]{1,0:T(8,128)(2,1)S(1)} %copy-done.15, f32[320]{0:T(512)S(1)} %copy-done.18), kind=kOutput, calls=%fused_computation.16 | convolution fusion | flops 3365928960 | bytes 21177600 | tf_op jit(solution)/shard_map/dot_general | solution.py:97
  129.5 12.1 %copy_bitcast_fusion = (bf16[8,2048,320]{1,2,0:T(8,128)(2,1)}, bf16[8,2048,320]{1,2,0:T(8,128)(2,1)}) fusion(bf16[40,8,8,2048]{3,2,1,0:T(8,128)(2,1)} %bitcast.72, bf16[40,8,8,2048]{3,2,1,0:T(8,128)(2,1)S(1)} %bitcast.67), kind=kLoop, calls=%fused_computation.18 | loop fusion | bytes 41943040
  141.6 225.4 %while.15 = (s32[]{:T(128)}, f32[5,512]{1,0:T(8,128)S(1)}, f32[5,512]{1,0:T(8,128)S(1)}, f32[5,512,64]{1,2,0:T(8,128)S(1)}, bf16[8,2048,320]{1,2,0:T(8,128)(2,1)...) while((s32[]{:T(128)}, f32[5,512]{1,0:T(8,128)S(1)}, ...), condition=%wide.region_7.8_spmd.clone, body=%wide.region_4.7_spmd.clone.sunk | while | flops 1368896000 | bytes 72581232 | solution.py:105
  141.6 2.0 constant_dynamic-slice_fusion.3
  143.6 8.6 %bitcast_reduce_fusion.2 = (f32[5,512]{1,0:T(8,128)S(1)}, f32[5,2048,512]{2,1,0:T(8,128)}) fusion(bf16[2048,5,64]{0,2,1:T(8,128)(2,1)S(1)} %bitcast.65, bf16[512,5,64]{0,2,1:T(8,128)(2,1)S(1)} %get-tuple-element.216), kind=kOutput, calls=%fused_computation.1.clone.1 | convolution fusion | flops 676328960 | bytes 22620160 | tf_op jit(solution)/shard_map/while/body/eval_jaxpr/qhd,khd->hqk/dot_general | solution.py:75
  152.2 8.8 %fusion.70 = f32[5,512]{1,0:T(8,128)S(1)} fusion(f32[5,2048,512]{2,1,0:T(8,128)} %get-tuple-element.189, f32[5,512]{1,0:T(8,128)S(1)} %select_maximum_fusion.2), kind=kLoop, calls=%fused_computation.4.clone.1 | loop fusion | flops 10483200 | bytes 20992000 | tf_op jit(solution)/shard_map/while/body/eval_jaxpr/reduce_sum | solution.py:79
  161.0 8.7 %fusion.72 = f32[5,512,64]{1,2,0:T(8,128)S(1)} fusion(bf16[2048,5,64]{0,2,1:T(8,128)(2,1)S(1)} %bitcast.66, f32[5,2048,512]{2,1,0:T(8,128)} %get-tuple-element.189, f32[5,512]{1,0:T(8,128)S(1)} %select_maximum_fusion.2, f32[5,512,64]{1,2,0:T(8,128)S(1)} %get-tuple-element.205, f32[5,512]{1,0:T(8,128)S(1)} %get-tuple-element.192, pred[]{:T(512)S(6)} %compare.3), kind=kOutput, calls=%fused_computation.7.clone.1 | convolution fusion | flops 682065920 | bytes 23613440 | tf_op jit(solution)/shard_map/while/body/eval_jaxpr/hqk,khd->hqd/dot_general | solution.py:80
  169.8 2.0 constant_dynamic-slice_fusion.3
  171.7 8.6 %bitcast_reduce_fusion.2 = (f32[5,512]{1,0:T(8,128)S(1)}, f32[5,2048,512]{2,1,0:T(8,128)}) fusion(bf16[2048,5,64]{0,2,1:T(8,128)(2,1)S(1)} %bitcast.65, bf16[512,5,64]{0,2,1:T(8,128)(2,1)S(1)} %get-tuple-element.216), kind=kOutput, calls=%fused_computation.1.clone.1 | convolution fusion | flops 676328960 | bytes 22620160 | tf_op jit(solution)/shard_map/while/body/eval_jaxpr/qhd,khd->hqk/dot_general | solution.py:75
  180.4 8.8 %fusion.70 = f32[5,512]{1,0:T(8,128)S(1)} fusion(f32[5,2048,512]{2,1,0:T(8,128)} %get-tuple-element.189, f32[5,512]{1,0:T(8,128)S(1)} %select_maximum_fusion.2), kind=kLoop, calls=%fused_computation.4.clone.1 | loop fusion | flops 10483200 | bytes 20992000 | tf_op jit(solution)/shard_map/while/body/eval_jaxpr/reduce_sum | solution.py:79
  189.2 8.7 %fusion.72 = f32[5,512,64]{1,2,0:T(8,128)S(1)} fusion(bf16[2048,5,64]{0,2,1:T(8,128)(2,1)S(1)} %bitcast.66, f32[5,2048,512]{2,1,0:T(8,128)} %get-tuple-element.189, f32[5,512]{1,0:T(8,128)S(1)} %select_maximum_fusion.2, f32[5,512,64]{1,2,0:T(8,128)S(1)} %get-tuple-element.205, f32[5,512]{1,0:T(8,128)S(1)} %get-tuple-element.192, pred[]{:T(512)S(6)} %compare.3), kind=kOutput, calls=%fused_computation.7.clone.1 | convolution fusion | flops 682065920 | bytes 23613440 | tf_op jit(solution)/shard_map/while/body/eval_jaxpr/hqk,khd->hqd/dot_general | solution.py:80
  197.9 2.0 constant_dynamic-slice_fusion.3
  199.9 8.6 %bitcast_reduce_fusion.2 = (f32[5,512]{1,0:T(8,128)S(1)}, f32[5,2048,512]{2,1,0:T(8,128)}) fusion(bf16[2048,5,64]{0,2,1:T(8,128)(2,1)S(1)} %bitcast.65, bf16[512,5,64]{0,2,1:T(8,128)(2,1)S(1)} %get-tuple-element.216), kind=kOutput, calls=%fused_computation.1.clone.1 | convolution fusion | flops 676328960 | bytes 22620160 | tf_op jit(solution)/shard_map/while/body/eval_jaxpr/qhd,khd->hqk/dot_general | solution.py:75
  208.5 8.8 %fusion.70 = f32[5,512]{1,0:T(8,128)S(1)} fusion(f32[5,2048,512]{2,1,0:T(8,128)} %get-tuple-element.189, f32[5,512]{1,0:T(8,128)S(1)} %select_maximum_fusion.2), kind=kLoop, calls=%fused_computation.4.clone.1 | loop fusion | flops 10483200 | bytes 20992000 | tf_op jit(solution)/shard_map/while/body/eval_jaxpr/reduce_sum | solution.py:79
  217.4 8.7 %fusion.72 = f32[5,512,64]{1,2,0:T(8,128)S(1)} fusion(bf16[2048,5,64]{0,2,1:T(8,128)(2,1)S(1)} %bitcast.66, f32[5,2048,512]{2,1,0:T(8,128)} %get-tuple-element.189, f32[5,512]{1,0:T(8,128)S(1)} %select_maximum_fusion.2, f32[5,512,64]{1,2,0:T(8,128)S(1)} %get-tuple-element.205, f32[5,512]{1,0:T(8,128)S(1)} %get-tuple-element.192, pred[]{:T(512)S(6)} %compare.3), kind=kOutput, calls=%fused_computation.7.clone.1 | convolution fusion | flops 682065920 | bytes 23613440 | tf_op jit(solution)/shard_map/while/body/eval_jaxpr/hqk,khd->hqd/dot_general | solution.py:80
  226.1 2.0 constant_dynamic-slice_fusion.3
  228.1 8.6 %bitcast_reduce_fusion.2 = (f32[5,512]{1,0:T(8,128)S(1)}, f32[5,2048,512]{2,1,0:T(8,128)}) fusion(bf16[2048,5,64]{0,2,1:T(8,128)(2,1)S(1)} %bitcast.65, bf16[512,5,64]{0,2,1:T(8,128)(2,1)S(1)} %get-tuple-element.216), kind=kOutput, calls=%fused_computation.1.clone.1 | convolution fusion | flops 676328960 | bytes 22620160 | tf_op jit(solution)/shard_map/while/body/eval_jaxpr/qhd,khd->hqk/dot_general | solution.py:75
  236.7 8.8 %fusion.70 = f32[5,512]{1,0:T(8,128)S(1)} fusion(f32[5,2048,512]{2,1,0:T(8,128)} %get-tuple-element.189, f32[5,512]{1,0:T(8,128)S(1)} %select_maximum_fusion.2), kind=kLoop, calls=%fused_computation.4.clone.1 | loop fusion | flops 10483200 | bytes 20992000 | tf_op jit(solution)/shard_map/while/body/eval_jaxpr/reduce_sum | solution.py:79
  245.5 8.7 %fusion.72 = f32[5,512,64]{1,2,0:T(8,128)S(1)} fusion(bf16[2048,5,64]{0,2,1:T(8,128)(2,1)S(1)} %bitcast.66, f32[5,2048,512]{2,1,0:T(8,128)} %get-tuple-element.189, f32[5,512]{1,0:T(8,128)S(1)} %select_maximum_fusion.2, f32[5,512,64]{1,2,0:T(8,128)S(1)} %get-tuple-element.205, f32[5,512]{1,0:T(8,128)S(1)} %get-tuple-element.192, pred[]{:T(512)S(6)} %compare.3), kind=kOutput, calls=%fused_computation.7.clone.1 | convolution fusion | flops 682065920 | bytes 23613440 | tf_op jit(solution)/shard_map/while/body/eval_jaxpr/hqk,khd->hqd/dot_general | solution.py:80
  254.3 2.0 constant_dynamic-slice_fusion.3
  256.2 8.6 %bitcast_reduce_fusion.2 = (f32[5,512]{1,0:T(8,128)S(1)}, f32[5,2048,512]{2,1,0:T(8,128)}) fusion(bf16[2048,5,64]{0,2,1:T(8,128)(2,1)S(1)} %bitcast.65, bf16[512,5,64]{0,2,1:T(8,128)(2,1)S(1)} %get-tuple-element.216), kind=kOutput, calls=%fused_computation.1.clone.1 | convolution fusion | flops 676328960 | bytes 22620160 | tf_op jit(solution)/shard_map/while/body/eval_jaxpr/qhd,khd->hqk/dot_general | solution.py:75
  264.9 8.8 %fusion.70 = f32[5,512]{1,0:T(8,128)S(1)} fusion(f32[5,2048,512]{2,1,0:T(8,128)} %get-tuple-element.189, f32[5,512]{1,0:T(8,128)S(1)} %select_maximum_fusion.2), kind=kLoop, calls=%fused_computation.4.clone.1 | loop fusion | flops 10483200 | bytes 20992000 | tf_op jit(solution)/shard_map/while/body/eval_jaxpr/reduce_sum | solution.py:79
  273.7 8.7 %fusion.72 = f32[5,512,64]{1,2,0:T(8,128)S(1)} fusion(bf16[2048,5,64]{0,2,1:T(8,128)(2,1)S(1)} %bitcast.66, f32[5,2048,512]{2,1,0:T(8,128)} %get-tuple-element.189, f32[5,512]{1,0:T(8,128)S(1)} %select_maximum_fusion.2, f32[5,512,64]{1,2,0:T(8,128)S(1)} %get-tuple-element.205, f32[5,512]{1,0:T(8,128)S(1)} %get-tuple-element.192, pred[]{:T(512)S(6)} %compare.3), kind=kOutput, calls=%fused_computation.7.clone.1 | convolution fusion | flops 682065920 | bytes 23613440 | tf_op jit(solution)/shard_map/while/body/eval_jaxpr/hqk,khd->hqd/dot_general | solution.py:80
  282.4 2.0 constant_dynamic-slice_fusion.3
  284.4 8.6 %bitcast_reduce_fusion.2 = (f32[5,512]{1,0:T(8,128)S(1)}, f32[5,2048,512]{2,1,0:T(8,128)}) fusion(bf16[2048,5,64]{0,2,1:T(8,128)(2,1)S(1)} %bitcast.65, bf16[512,5,64]{0,2,1:T(8,128)(2,1)S(1)} %get-tuple-element.216), kind=kOutput, calls=%fused_computation.1.clone.1 | convolution fusion | flops 676328960 | bytes 22620160 | tf_op jit(solution)/shard_map/while/body/eval_jaxpr/qhd,khd->hqk/dot_general | solution.py:75
  293.1 8.8 %fusion.70 = f32[5,512]{1,0:T(8,128)S(1)} fusion(f32[5,2048,512]{2,1,0:T(8,128)} %get-tuple-element.189, f32[5,512]{1,0:T(8,128)S(1)} %select_maximum_fusion.2), kind=kLoop, calls=%fused_computation.4.clone.1 | loop fusion | flops 10483200 | bytes 20992000 | tf_op jit(solution)/shard_map/while/body/eval_jaxpr/reduce_sum | solution.py:79
  301.9 8.7 %fusion.72 = f32[5,512,64]{1,2,0:T(8,128)S(1)} fusion(bf16[2048,5,64]{0,2,1:T(8,128)(2,1)S(1)} %bitcast.66, f32[5,2048,512]{2,1,0:T(8,128)} %get-tuple-element.189, f32[5,512]{1,0:T(8,128)S(1)} %select_maximum_fusion.2, f32[5,512,64]{1,2,0:T(8,128)S(1)} %get-tuple-element.205, f32[5,512]{1,0:T(8,128)S(1)} %get-tuple-element.192, pred[]{:T(512)S(6)} %compare.3), kind=kOutput, calls=%fused_computation.7.clone.1 | convolution fusion | flops 682065920 | bytes 23613440 | tf_op jit(solution)/shard_map/while/body/eval_jaxpr/hqk,khd->hqd/dot_general | solution.py:80
  310.6 2.0 constant_dynamic-slice_fusion.3
  312.6 8.6 %bitcast_reduce_fusion.2 = (f32[5,512]{1,0:T(8,128)S(1)}, f32[5,2048,512]{2,1,0:T(8,128)}) fusion(bf16[2048,5,64]{0,2,1:T(8,128)(2,1)S(1)} %bitcast.65, bf16[512,5,64]{0,2,1:T(8,128)(2,1)S(1)} %get-tuple-element.216), kind=kOutput, calls=%fused_computation.1.clone.1 | convolution fusion | flops 676328960 | bytes 22620160 | tf_op jit(solution)/shard_map/while/body/eval_jaxpr/qhd,khd->hqk/dot_general | solution.py:75
  321.2 8.8 %fusion.70 = f32[5,512]{1,0:T(8,128)S(1)} fusion(f32[5,2048,512]{2,1,0:T(8,128)} %get-tuple-element.189, f32[5,512]{1,0:T(8,128)S(1)} %select_maximum_fusion.2), kind=kLoop, calls=%fused_computation.4.clone.1 | loop fusion | flops 10483200 | bytes 20992000 | tf_op jit(solution)/shard_map/while/body/eval_jaxpr/reduce_sum | solution.py:79
  330.0 8.7 %fusion.72 = f32[5,512,64]{1,2,0:T(8,128)S(1)} fusion(bf16[2048,5,64]{0,2,1:T(8,128)(2,1)S(1)} %bitcast.66, f32[5,2048,512]{2,1,0:T(8,128)} %get-tuple-element.189, f32[5,512]{1,0:T(8,128)S(1)} %select_maximum_fusion.2, f32[5,512,64]{1,2,0:T(8,128)S(1)} %get-tuple-element.205, f32[5,512]{1,0:T(8,128)S(1)} %get-tuple-element.192, pred[]{:T(512)S(6)} %compare.3), kind=kOutput, calls=%fused_computation.7.clone.1 | convolution fusion | flops 682065920 | bytes 23613440 | tf_op jit(solution)/shard_map/while/body/eval_jaxpr/hqk,khd->hqd/dot_general | solution.py:80
  338.8 2.0 constant_dynamic-slice_fusion.3
  340.8 8.6 %bitcast_reduce_fusion.2 = (f32[5,512]{1,0:T(8,128)S(1)}, f32[5,2048,512]{2,1,0:T(8,128)}) fusion(bf16[2048,5,64]{0,2,1:T(8,128)(2,1)S(1)} %bitcast.65, bf16[512,5,64]{0,2,1:T(8,128)(2,1)S(1)} %get-tuple-element.216), kind=kOutput, calls=%fused_computation.1.clone.1 | convolution fusion | flops 676328960 | bytes 22620160 | tf_op jit(solution)/shard_map/while/body/eval_jaxpr/qhd,khd->hqk/dot_general | solution.py:75
  349.4 8.8 %fusion.70 = f32[5,512]{1,0:T(8,128)S(1)} fusion(f32[5,2048,512]{2,1,0:T(8,128)} %get-tuple-element.189, f32[5,512]{1,0:T(8,128)S(1)} %select_maximum_fusion.2), kind=kLoop, calls=%fused_computation.4.clone.1 | loop fusion | flops 10483200 | bytes 20992000 | tf_op jit(solution)/shard_map/while/body/eval_jaxpr/reduce_sum | solution.py:79
  358.2 8.7 %fusion.72 = f32[5,512,64]{1,2,0:T(8,128)S(1)} fusion(bf16[2048,5,64]{0,2,1:T(8,128)(2,1)S(1)} %bitcast.66, f32[5,2048,512]{2,1,0:T(8,128)} %get-tuple-element.189, f32[5,512]{1,0:T(8,128)S(1)} %select_maximum_fusion.2, f32[5,512,64]{1,2,0:T(8,128)S(1)} %get-tuple-element.205, f32[5,512]{1,0:T(8,128)S(1)} %get-tuple-element.192, pred[]{:T(512)S(6)} %compare.3), kind=kOutput, calls=%fused_computation.7.clone.1 | convolution fusion | flops 682065920 | bytes 23613440 | tf_op jit(solution)/shard_map/while/body/eval_jaxpr/hqk,khd->hqd/dot_general | solution.py:80
  367.1 1.5 fusion.43
  368.8 1.0 fusion.11
  369.8 4.0 collective-permute-start.1
  373.8 2.8 collective-permute-start
  376.6 4.4 %collective-permute-done = bf16[1,16,1280]{2,1,0:T(8,128)(2,1)S(1)} collective-permute-done((bf16[1,16,1280]{2,1,0:T(8,128)(2,1)S(1)}, bf16[1,16,1280]{2,1,0:T(8,128)(2,1)S(1)}, u32[]{:S(2)}, u32[]{:S(2)}) %collective-permute-start) | collective-permute-done | bytes 40992 | tf_op jit(solution)/shard_map/ppermute | solution.py:16
  381.0 0.3 pad_maximum_fusion.5
  381.2 5.7 %collective-permute-start.2 = (bf16[34,1,1280]{2,1,0:T(2,128)(2,1)S(1)}, bf16[34,1,1280]{2,1,0:T(2,128)(2,1)S(1)}, u32[]{:S(2)}, u32[]{:S(2)}) collective-permute-start(bf16[34,1,1280]{2,1,0:T(2,128)(2,1)S(1)} %get-tuple-element.128), channel_id=1, source_target_pairs={{0,1},{1,2},{2,3},{3,4},{4,5},{5,6},{6,7},{7,8},{8,9},{9,10},{10,1... | collective-permute-start | bytes 261128 | tf_op jit(solution)/shard_map/ppermute | solution.py:16
  387.0 1.9 collective-permute-start.3
  389.1 0.3 collective-permute-done.2
  389.3 5.3 %collective-permute-done.3 = bf16[34,1,1280]{2,1,0:T(2,128)(2,1)S(1)} collective-permute-done((bf16[34,1,1280]{2,1,0:T(2,128)(2,1)S(1)}, bf16[34,1,1280]{2,1,0:T(2,128)(2,1)S(1)}, u32[]{:S(2)}, u32[]{:S(2)}) %collective-permute-start.3) | collective-permute-done | bytes 87072 | tf_op jit(solution)/shard_map/ppermute | solution.py:17
  394.6 1.3 maximum_maximum_fusion
  395.9 9.0 %fusion.14 = bf16[32,16,1280]{2,1,0:T(8,128)(2,1)S(1)} fusion(bf16[32,16,1280]{2,1,0:T(8,128)(2,1)S(1)} %bitcast.71, bf16[34,17,1280]{2,1,0:T(8,128)(2,1)S(1)} %get-tuple-element.127, bf16[1,16,1280]{2,1,0:T(8,128)(2,1)S(1)} %collective-permute-done.1, bf16[34,17,1280]{2,1,0:T(8,128)(2,1)S(1)} %get-tuple-element.126, ...), kind=kLoop, calls=%fused_computation.25 | loop fusion | flops 61603840 | bytes 10618880 | tf_op jit(solution)/shard_map/convert_element_type | solution.py:134
  405.0 0.6 fusion.28
  405.6 0.9 copy.58
  (90 shorter events, 1.2 us)
Async XLA Ops:
  6.5 362.2 %copy-start = (bf16[320,1280]{1,0:T(8,128)(2,1)S(1)}, bf16[320,1280]{1,0:T(8,128)(2,1)}, u32[]{:S(2)}) copy-start(bf16[320,1280]{1,0:T(8,128)(2,1)} %param.40) | copy-start | bytes 2457604
  6.5 4.8 %copy-start.10 = (f32[320]{0:T(512)S(1)}, f32[320]{0:T(512)}, u32[]{:S(2)}) copy-start(f32[320]{0:T(512)} %param.26) | copy-start | bytes 3844
  6.5 4.8 %copy-start.11 = (f32[320]{0:T(512)S(1)}, f32[320]{0:T(512)}, u32[]{:S(2)}) copy-start(f32[320]{0:T(512)} %param.25) | copy-start | bytes 3844
  6.5 5.7 %copy-start.7 = (f32[320]{0:T(512)S(1)}, f32[320]{0:T(512)}, u32[]{:S(2)}) copy-start(f32[320]{0:T(512)} %param.30) | copy-start | bytes 3844
  6.5 5.7 %copy-start.2 = (bf16[1280,320]{0,1:T(8,128)(2,1)S(1)}, bf16[1280,320]{0,1:T(8,128)(2,1)}, u32[]{:S(2)}) copy-start(bf16[1280,320]{0,1:T(8,128)(2,1)} %param.29) | copy-start | bytes 2457604
  6.5 103.9 %all-gather.2.cloned.1.call-start = ((), (), s32[]{:S(2)}) async-start(), calls=%async_computation | async-start | bytes 11141120 | tf_op jit(solution)/shard_map/all_gather | solution.py:94
  9.3 3.4 copy-start.8
  9.3 3.4 copy-start.9
  11.6 29.7 %copy-start.1 = (bf16[32,16,320]{2,1,0:T(8,128)(2,1)S(1)}, bf16[32,16,320]{2,1,0:T(8,128)(2,1)}, u32[]{:S(2)}) copy-start(bf16[32,16,320]{2,1,0:T(8,128)(2,1)} %param.24) | copy-start | bytes 983044
  12.2 30.4 %copy-start.14 = (bf16[320,320]{1,0:T(8,128)(2,1)S(1)}, bf16[320,320]{1,0:T(8,128)(2,1)}, u32[]{:S(2)}) copy-start(bf16[320,320]{1,0:T(8,128)(2,1)} %param.27) | copy-start | bytes 614404
  12.2 30.4 %copy-start.17 = (f32[320]{0:T(512)S(1)}, f32[320]{0:T(512)}, u32[]{:S(2)}) copy-start(f32[320]{0:T(512)} %param.28) | copy-start | bytes 3844
  41.2 69.2 %copy-start.4 = (bf16[320,320]{1,0:T(8,128)(2,1)S(1)}, bf16[320,320]{1,0:T(8,128)(2,1)}, u32[]{:S(2)}) copy-start(bf16[320,320]{1,0:T(8,128)(2,1)} %param.33) | copy-start | bytes 614404
  43.2 75.7 %copy-start.15 = (bf16[320,320]{1,0:T(8,128)(2,1)S(1)}, bf16[320,320]{1,0:T(8,128)(2,1)}, u32[]{:S(2)}) copy-start(bf16[320,320]{1,0:T(8,128)(2,1)} %param.34) | copy-start | bytes 614404
  43.2 75.7 %copy-start.18 = (f32[320]{0:T(512)S(1)}, f32[320]{0:T(512)}, u32[]{:S(2)}) copy-start(f32[320]{0:T(512)} %param.35) | copy-start | bytes 3844
  141.6 225.5 %copy-start.3 = (bf16[320,320]{1,0:T(8,128)(2,1)S(1)}, bf16[320,320]{1,0:T(8,128)(2,1)}, u32[]{:S(2)}) copy-start(bf16[320,320]{1,0:T(8,128)(2,1)} %param.36) | copy-start | bytes 614404
  141.6 225.5 %copy-start.12 = (f32[320]{0:T(512)S(1)}, f32[320]{0:T(512)}, u32[]{:S(2)}) copy-start(f32[320]{0:T(512)} %param.37) | copy-start | bytes 3844
  366.9 1.8 copy-start.16
  367.0 1.8 copy-start.19
  367.0 1.8 copy-start.20
  368.7 20.2 %copy-start.5 = (f32[9,1280]{1,0:T(8,128)S(1)}, f32[9,1280]{1,0:T(8,128)}, u32[]{:S(2)}) copy-start(f32[9,1280]{1,0:T(8,128)} %param.42) | copy-start | bytes 138244
  369.8 6.8 %collective-permute-start.1 = (bf16[1,16,1280]{2,1,0:T(8,128)(2,1)S(1)}, bf16[1,16,1280]{2,1,0:T(8,128)(2,1)S(1)}, u32[]{:S(2)}, u32[]{:S(2)}) collective-permute-start(bf16[1,16,1280]{2,1,0:T(8,128)(2,1)S(1)} %get-tuple-element.131), channel_id=1, source_target_pairs={{16,0},{32,16},{48,32},{64,48},{80,64},{96,80},{112,96},{17,1},{33... | collective-permute-start | bytes 122888 | tf_op jit(solution)/shard_map/ppermute | solution.py:17
  373.8 7.1 %collective-permute-start = (bf16[1,16,1280]{2,1,0:T(8,128)(2,1)S(1)}, bf16[1,16,1280]{2,1,0:T(8,128)(2,1)S(1)}, u32[]{:S(2)}, u32[]{:S(2)}) collective-permute-start(bf16[1,16,1280]{2,1,0:T(8,128)(2,1)S(1)} %get-tuple-element.130), channel_id=1, source_target_pairs={{0,16},{16,32},{32,48},{48,64},{64,80},{80,96},{96,112},{1,17},{17... | collective-permute-start | bytes 122888 | tf_op jit(solution)/shard_map/ppermute | solution.py:16
  381.2 8.1 %collective-permute-start.2 = (bf16[34,1,1280]{2,1,0:T(2,128)(2,1)S(1)}, bf16[34,1,1280]{2,1,0:T(2,128)(2,1)S(1)}, u32[]{:S(2)}, u32[]{:S(2)}) collective-permute-start(bf16[34,1,1280]{2,1,0:T(2,128)(2,1)S(1)} %get-tuple-element.128), channel_id=1, source_target_pairs={{0,1},{1,2},{2,3},{3,4},{4,5},{5,6},{6,7},{7,8},{8,9},{9,10},{10,1... | collective-permute-start | bytes 261128 | tf_op jit(solution)/shard_map/ppermute | solution.py:16
  387.0 7.6 %collective-permute-start.3 = (bf16[34,1,1280]{2,1,0:T(2,128)(2,1)S(1)}, bf16[34,1,1280]{2,1,0:T(2,128)(2,1)S(1)}, u32[]{:S(2)}, u32[]{:S(2)}) collective-permute-start(bf16[34,1,1280]{2,1,0:T(2,128)(2,1)S(1)} %get-tuple-element.129), channel_id=1, source_target_pairs={{1,0},{2,1},{3,2},{4,3},{5,4},{6,5},{7,6},{8,7},{9,8},{10,9},{11,1... | collective-permute-start | bytes 261128 | tf_op jit(solution)/shard_map/ppermute | solution.py:17
  389.1 6.8 %copy-start.6 = (f32[1280]{0:T(1024)S(1)}, f32[1280]{0:T(1024)}, u32[]{:S(2)}) copy-start(f32[1280]{0:T(1024)} %param.43) | copy-start | bytes 15364
  395.9 9.0 %copy-start.13 = (bf16[1280,320]{0,1:T(8,128)(2,1)S(1)}, bf16[1280,320]{0,1:T(8,128)(2,1)}, u32[]{:S(2)}) copy-start(bf16[1280,320]{0,1:T(8,128)(2,1)} %param.44) | copy-start | bytes 2457604
  395.9 9.0 %copy-start.21 = (f32[320]{0:T(512)S(1)}, f32[320]{0:T(512)}, u32[]{:S(2)}) copy-start(f32[320]{0:T(512)} %param.45) | copy-start | bytes 3844
Sparse Core Ops, SparseCore 0:
  41.4 69.0 all-gather.1

commit v2 on v1

--- a/solution.py
+++ b/solution.py
@@ -2,6 +2,8 @@
 import jax.numpy as jnp
 from jax import lax
 from jax.sharding import PartitionSpec as P
+from jax.experimental import pallas as pl
+from jax.experimental.pallas import tpu as pltpu
 
 HEADS = 5
 
@@ -24,6 +26,66 @@
     centered = value - mean
     var = jnp.mean(centered * centered, axis=-1, keepdims=True)
     return centered * lax.rsqrt(var + 1e-06) * gain + shift
+
+
+KV_BLOCK = 512
+
+
+def attend_kernel(q_ref, rn_ref, wk_ref, wv_ref, bv_ref, o_ref, m_ref, l_ref, acc_ref):
+    step = pl.program_id(0)
+
+    @pl.when(step == 0)
+    def _():
+        m_ref[...] = jnp.full(m_ref.shape, -1e30, jnp.float32)
+        l_ref[...] = jnp.zeros(l_ref.shape, jnp.float32)
+        acc_ref[...] = jnp.zeros(acc_ref.shape, jnp.float32)
+
+    rn = rn_ref[...]
+    for h in range(HEADS):
+        k_h = jnp.dot(rn, wk_ref[h], preferred_element_type=jnp.float32).astype(jnp.bfloat16)
+        v_h = (jnp.dot(rn, wv_ref[h], preferred_element_type=jnp.float32) + bv_ref[h]).astype(
+            jnp.bfloat16
+        )
+        scores = lax.dot_general(
+            q_ref[h], k_h, (((1,), (1,)), ((), ())), preferred_element_type=jnp.float32
+        )
+        run_max = m_ref[h]
+        new_max = jnp.maximum(run_max, jnp.max(scores, axis=-1, keepdims=True))
+        factor = jnp.exp(run_max - new_max)
+        expo = jnp.exp(scores - new_max)
+        l_ref[h] = l_ref[h] * factor + jnp.sum(expo, axis=-1, keepdims=True)
+        acc_ref[h] = acc_ref[h] * factor + jnp.dot(
+            expo.astype(jnp.bfloat16), v_h, preferred_element_type=jnp.float32
+        )
+        m_ref[h] = new_max
+
+    @pl.when(step == pl.num_programs(0) - 1)
+    def _():
+        o_ref[...] = (acc_ref[...] / l_ref[...]).astype(o_ref.dtype)
+
+
+def attend(query_heads, gathered, wk_heads, wv_heads, bv_heads):
+    heads, count, head_dim = query_heads.shape
+    length, chans = gathered.shape
+    return pl.pallas_call(
+        attend_kernel,
+        grid=(length // KV_BLOCK,),
+        in_specs=[
+            pl.BlockSpec((heads, count, head_dim), lambda j: (0, 0, 0)),
+            pl.BlockSpec((KV_BLOCK, chans), lambda j: (j, 0)),
+            pl.BlockSpec((heads, chans, head_dim), lambda j: (0, 0, 0)),
+            pl.BlockSpec((heads, chans, head_dim), lambda j: (0, 0, 0)),
+            pl.BlockSpec((heads, 1, head_dim), lambda j: (0, 0, 0)),
+        ],
+        out_specs=pl.BlockSpec((heads, count, head_dim), lambda j: (0, 0, 0)),
+        out_shape=jax.ShapeDtypeStruct((heads, count, head_dim), jnp.bfloat16),
+        scratch_shapes=[
+            pltpu.VMEM((heads, count, 1), jnp.float32),
+            pltpu.VMEM((heads, count, 1), jnp.float32),
+            pltpu.VMEM((heads, count, head_dim), jnp.float32),
+        ],
+        compiler_params=pltpu.CompilerParams(dimension_semantics=("arbitrary",)),
+    )(query_heads, gathered, wk_heads, wv_heads, bv_heads)
 
 
 def per_device(
@@ -68,52 +130,13 @@
     reduced = jnp.dot(blocks, w_reduce, preferred_element_type=jnp.float32) + b_reduce
     reduced_norm = layer_norm(reduced, reduce_gain, reduce_shift).astype(jnp.bfloat16)
 
-    def one_block(carry, keys, values):
-        run_max, run_sum, accum = carry
-        key_heads = keys.reshape(-1, HEADS, head_dim)
-        value_heads = values.reshape(-1, HEADS, head_dim)
-        scores = jnp.einsum("qhd,khd->hqk", query, key_heads, preferred_element_type=jnp.float32)
-        new_max = jnp.maximum(run_max, jnp.max(scores, axis=-1))
-        factor = jnp.exp(run_max - new_max)
-        expo = jnp.exp(scores - new_max[..., None])
-        run_sum = run_sum * factor + jnp.sum(expo, axis=-1)
-        accum = accum * factor[..., None] + jnp.einsum(
-            "hqk,khd->hqd",
-            expo.astype(jnp.bfloat16),
-            value_heads,
-            preferred_element_type=jnp.float32,
-        )
-        return (new_max, run_sum, accum)
-
-    start_state = (
-        jnp.full((HEADS, count), -1e30, jnp.float32),
-        jnp.zeros((HEADS, count), jnp.float32),
-        jnp.zeros((HEADS, count, head_dim), jnp.float32),
-    )
     gathered = lax.all_gather(reduced_norm, "rows", axis=0, tiled=True)
     gathered = lax.all_gather(gathered, "cols", axis=0, tiled=True)
-    attend_keys = jnp.dot(gathered, w_key, preferred_element_type=jnp.float32).astype(jnp.bfloat16)
-    attend_values = (
-        jnp.dot(gathered, w_value, preferred_element_type=jnp.float32) + b_value
-    ).astype(jnp.bfloat16)
-    carry = start_state
-    length = attend_keys.shape[0]
-
-    def step(state, pair):
-        return (one_block(state, pair[0], pair[1]), None)
-
-    carry, unused = lax.scan(
-        step,
-        carry,
-        (
-            attend_keys.reshape(length // 2048, 2048, chans),
-            attend_values.reshape(length // 2048, 2048, chans),
-        ),
-    )
-    run_max, run_sum, accum = carry
-    attended = (
-        (accum / run_sum[..., None]).transpose(1, 0, 2).reshape(count, chans).astype(jnp.bfloat16)
-    )
+    wk_heads = w_key.reshape(chans, HEADS, head_dim).transpose(1, 0, 2)
+    wv_heads = w_value.reshape(chans, HEADS, head_dim).transpose(1, 0, 2)
+    bv_heads = b_value.reshape(HEADS, 1, head_dim)
+    attended = attend(query.transpose(1, 0, 2), gathered, wk_heads, wv_heads, bv_heads)
+    attended = attended.transpose(1, 0, 2).reshape(count, chans)
     mid = (flat + jnp.dot(attended, w_out, preferred_element_type=jnp.float32) + b_out).astype(
         jnp.bfloat16
     )

time: 414 us -> 372 us (0.90)
  Pallas kernels: 0 us -> 199 us
  matrix products: 162 us -> 3.08 us
  other arithmetic: 84.1 us -> 13.7 us
  local copies, waits for them, and re-layouts: 33.1 us -> 9.74 us
  waiting for transfers between devices: 77.2 us -> 86 us
    pallas_call x0 -> x1, Pallas kernels: none -> 199 us  [attend(): pl.pallas_call(attend_kernel, grid=(length // KV_BLOCK,), in_specs=[pl.Bl...]
    dot_general x18 -> x0, matrix products: 158 us -> none  [the longest x8 69.8 us: one_block(): jnp.einsum('hqk,khd->hqd', expo.astype(jnp.bfloat16), value_heads, prefer...]
    reduce_sum x8 -> x0, other arithmetic: 70.3 us -> none  [one_block(): run_sum = run_sum * factor + jnp.sum(expo, axis=-1)]
    dynamic_slice x8 -> x0, local copies, waits for them, and re-layouts: 15.7 us -> none  [per_device(): lax.scan(step, carry, (attend_keys.reshape(length // 2048, 2048, chans),...]
    unnamed x45 -> x46, local copies, waits for them, and re-layouts: 12.2 us -> 0.5 us
    all_gather x1, waiting for transfers between devices: 67.3 us -> 76.2 us  [per_device(): gathered = lax.all_gather(gathered, 'cols', axis=0, tiled=True)]
  transfers between devices with their start and end apart: 5 -> 5, of which waited for: 4 -> 4; matrix products, arithmetic and copies ran while one was open for 0% -> 1% of each run, Pallas kernels for 0% -> 0%
where the time goes in v2:
time: 372 us; the launch traced here: 371 us
  Pallas kernels  199 us (53%)
  waiting for transfers between devices  86 us (23%)
  blocking collectives  30.8 us (8%)
  starting transfers between devices  14.7 us (4%)
  between operations  13.9 us (4%)
  other arithmetic  13.7 us (4%)
  local copies, waits for them, and re-layouts  9.74 us (3%)
    pallas_call x1, Pallas kernels, attend(): pl.pallas_call(attend_kernel, grid=(length // KV_BLOCK,), in_specs=[pl.Bl...  199 us
    all_gather x1, waiting for transfers between devices, per_device(): gathered = lax.all_gather(gathered, 'cols', axis=0, tiled=True)  76.2 us
    all_gather x1, blocking collectives, per_device(): gathered = lax.all_gather(reduced_norm, 'rows', axis=0, tiled=True)  30.8 us
    convert_element_type x1, other arithmetic, per_device(): jax.nn.gelu(spread, approximate=False).astype(jnp.bfloat16)  9 us
    ppermute x2, starting transfers between devices, padded_2(): before = lax.ppermute(last, axis, up)  8.69 us
  transfers between devices with their start and end apart: 5, of which 4 were waited for; matrix products, arithmetic and copies ran while one was open for 1% of the time, Pallas kernels for 0%

profile of v2, /device:TPU:15, one launch (start us, length us, event | category | flops | bytes accessed | tf_op | source)
XLA Modules:
  0.0 371.3 jit_solution(7244175837467632039)
XLA Ops:
  6.5 0.0 copy-start
  6.5 0.0 all-gather.2.cloned.1.call-start
  6.5 1.2 convert_reduce_fusion
  7.8 0.0 copy-start.2
  7.8 0.0 copy-start.8
  7.8 1.5 reshape.150
  9.3 0.0 copy-start.9
  9.3 0.0 copy-start.10
  9.3 1.3 multiply_reduce_fusion
  10.6 0.1 reshape.151
  10.7 0.1 reshape.152
  10.8 0.3 copy.74
  11.0 0.3 copy.71
  11.3 0.0 copy-done.11
  11.3 0.0 copy-done.12
  11.3 0.2 fusion.22
  11.6 0.0 copy-start.1
  11.6 0.3 copy.75
  11.9 0.3 reshape.141
  12.2 0.0 copy-done.2
  12.2 0.5 fusion.31
  12.8 0.0 copy-start.18
  12.8 0.2 multiply_reduce_fusion.2
  13.0 0.1 add_convert_fusion.4
  13.1 30.8 %all_gather.6 = bf16[1024,320]{1,0:T(8,128)(2,1)} all-gather(bf16[128,320]{1,0:T(8,128)(2,1)S(1)} %add_convert_fusion.4), channel_id=1, replica_groups=mesh['rows'=8,'cols'=16] {'rows'}, dimensions={0}, use_global_device_ids=true | all-gather | bytes 737280 | tf_op jit(solution)/shard_map/all_gather | solution.py:133
  43.9 0.0 all-gather.2.cloned.1.call-update
  43.9 0.0 copy-start.4
  44.0 0.1 convert_element_type.98
  44.0 0.1 rsqrt.32
  44.1 0.1 div.23
  44.2 0.3 copy.82
  44.5 0.0 copy-start.14
  44.5 0.5 fusion.14
  45.0 1.1 copy.69
  46.1 0.0 copy-done.4
  46.1 0.2 copy.77
  46.3 1.0 copy.78
  47.3 0.2 copy.79
  47.5 0.9 copy.80
  48.4 0.7 reshape.144.bv_ref
  49.0 76.2 %all-gather.2.cloned.1.call-done.rn_ref = bf16[16384,320]{1,0:T(8,128)(2,1)} async-done(((bf16[1024,320]{1,0:T(8,128)(2,1)}), bf16[16384,320]{1,0:T(8,128)(2,1)}) %all-gather.2.cloned.1.call-update) | async-done | bytes 10485776 | tf_op jit(solution)/shard_map/all_gather | solution.py:134
  125.3 199.4 %shard_map.208 = bf16[5,512,64]{2,1,0:T(8,128)(2,1)} custom-call(bf16[5,512,64]{2,1,0:T(8,128)(2,1)} %bitcast.31, bf16[16384,320]{1,0:T(8,128)(2,1)} %all-gather.2.cloned.1.call-done.rn_ref, bf16[5,320,64]{2,1,0:T(8,128)(2,1)} %bitcast.33, bf16[5,320,64]{2,1,0:T(8,128)(2,1)} %bitcast.34, f32[5,1,64]{2,1,0:T(1,128)} %reshape.144.bv_ref), custom_call_target="tpu_custom_call" | custom-call | tf_op jit(solution)/shard_map/pallas_call | solution.py:70
  324.7 1.3 copy.81
  326.1 0.4 fusion.32
  326.5 0.1 multiply_reduce_fusion.1
  326.7 0.0 copy-start.6
  326.7 1.0 fusion
  327.7 4.0 %collective-permute-start.1 = (bf16[1,16,1280]{2,1,0:T(8,128)(2,1)S(1)}, bf16[1,16,1280]{2,1,0:T(8,128)(2,1)S(1)}, u32[]{:S(2)}, u32[]{:S(2)}) collective-permute-start(bf16[1,16,1280]{2,1,0:T(8,128)(2,1)S(1)} %get-tuple-element.19), channel_id=1, source_target_pairs={{16,0},{32,16},{48,32},{64,48},{80,64},{96,80},{112,96},{17,1},{33... | collective-permute-start | bytes 122888 | tf_op jit(solution)/shard_map/ppermute | solution.py:19
  331.8 2.9 collective-permute-start
  334.7 0.0 collective-permute-done.1
  334.7 4.2 %collective-permute-done = bf16[1,16,1280]{2,1,0:T(8,128)(2,1)S(1)} collective-permute-done((bf16[1,16,1280]{2,1,0:T(8,128)(2,1)S(1)}, bf16[1,16,1280]{2,1,0:T(8,128)(2,1)S(1)}, u32[]{:S(2)}, u32[]{:S(2)}) %collective-permute-start) | collective-permute-done | bytes 40992 | tf_op jit(solution)/shard_map/ppermute | solution.py:18
  338.9 0.3 pad_maximum_fusion.5
  339.2 5.8 %collective-permute-start.2 = (bf16[34,1,1280]{2,1,0:T(2,128)(2,1)S(1)}, bf16[34,1,1280]{2,1,0:T(2,128)(2,1)S(1)}, u32[]{:S(2)}, u32[]{:S(2)}) collective-permute-start(bf16[34,1,1280]{2,1,0:T(2,128)(2,1)S(1)} %get-tuple-element.16), channel_id=1, source_target_pairs={{0,1},{1,2},{2,3},{3,4},{4,5},{5,6},{6,7},{7,8},{8,9},{9,10},{10,1... | collective-permute-start | bytes 261128 | tf_op jit(solution)/shard_map/ppermute | solution.py:18
  345.0 1.9 collective-permute-start.3
  346.9 0.1 slice_reduce_fusion.8
  347.0 0.0 copy-start.7
  347.0 0.3 collective-permute-done.2
  347.3 5.3 %collective-permute-done.3 = bf16[34,1,1280]{2,1,0:T(2,128)(2,1)S(1)} collective-permute-done((bf16[34,1,1280]{2,1,0:T(2,128)(2,1)S(1)}, bf16[34,1,1280]{2,1,0:T(2,128)(2,1)S(1)}, u32[]{:S(2)}, u32[]{:S(2)}) %collective-permute-start.3) | collective-permute-done | bytes 87072 | tf_op jit(solution)/shard_map/ppermute | solution.py:19
  352.6 1.3 maximum_maximum_fusion
  353.9 0.0 copy-start.15
  353.9 0.0 copy-start.21
  353.9 9.0 %fusion.3 = bf16[32,16,1280]{2,1,0:T(8,128)(2,1)S(1)} fusion(bf16[32,16,1280]{2,1,0:T(8,128)(2,1)S(1)} %bitcast.28, bf16[34,17,1280]{2,1,0:T(8,128)(2,1)S(1)} %get-tuple-element.15, bf16[1,16,1280]{2,1,0:T(8,128)(2,1)S(1)} %collective-permute-done.1, bf16[34,17,1280]{2,1,0:T(8,128)(2,1)S(1)} %get-tuple-element.14, ...), kind=kLoop, calls=%fused_computation.5 | loop fusion | flops 61603840 | bytes 10618880 | tf_op jit(solution)/shard_map/convert_element_type | solution.py:157
  362.9 0.6 fusion.17
  363.6 0.9 copy.83
  (34 shorter events, 0.1 us)
Async XLA Ops:
  6.5 320.1 %copy-start = (bf16[320,1280]{1,0:T(8,128)(2,1)S(1)}, bf16[320,1280]{1,0:T(8,128)(2,1)}, u32[]{:S(2)}) copy-start(bf16[320,1280]{1,0:T(8,128)(2,1)} %param.38) | copy-start | bytes 2457604
  6.5 4.8 %copy-start.11 = (f32[320]{0:T(512)S(1)}, f32[320]{0:T(512)}, u32[]{:S(2)}) copy-start(f32[320]{0:T(512)} %param.24) | copy-start | bytes 3844
  6.5 4.8 %copy-start.12 = (f32[320]{0:T(512)S(1)}, f32[320]{0:T(512)}, u32[]{:S(2)}) copy-start(f32[320]{0:T(512)} %param.23) | copy-start | bytes 3844
  6.5 118.7 %all-gather.2.cloned.1.call-start = ((), (), s32[]{:S(2)}) async-start(), calls=%async_computation | async-start | bytes 13369344 | tf_op jit(solution)/shard_map/all_gather | solution.py:134
  7.8 4.4 %copy-start.2 = (bf16[1280,320]{0,1:T(8,128)(2,1)S(1)}, bf16[1280,320]{0,1:T(8,128)(2,1)}, u32[]{:S(2)}) copy-start(bf16[1280,320]{0,1:T(8,128)(2,1)} %param.27) | copy-start | bytes 2457604
  7.8 4.4 %copy-start.8 = (f32[320]{0:T(512)S(1)}, f32[320]{0:T(512)}, u32[]{:S(2)}) copy-start(f32[320]{0:T(512)} %param.28) | copy-start | bytes 3844
  9.3 3.7 copy-start.9
  9.3 3.7 copy-start.10
  11.6 32.4 %copy-start.1 = (bf16[32,16,320]{2,1,0:T(8,128)(2,1)S(1)}, bf16[32,16,320]{2,1,0:T(8,128)(2,1)}, u32[]{:S(2)}) copy-start(bf16[32,16,320]{2,1,0:T(8,128)(2,1)} %param.22) | copy-start | bytes 983044
  12.7 31.7 %copy-start.16 = (bf16[320,320]{1,0:T(8,128)(2,1)S(1)}, bf16[320,320]{1,0:T(8,128)(2,1)}, u32[]{:S(2)}) copy-start(bf16[320,320]{1,0:T(8,128)(2,1)} %param.25) | copy-start | bytes 614404
  12.8 31.7 %copy-start.18 = (f32[320]{0:T(512)S(1)}, f32[320]{0:T(512)}, u32[]{:S(2)}) copy-start(f32[320]{0:T(512)} %param.26) | copy-start | bytes 3844
  43.9 2.2 copy-start.4
  44.2 3.1 copy-start.5
  44.5 3.9 %copy-start.14 = (f32[320]{0:T(512)S(1)}, f32[320]{0:T(512)}, u32[]{:S(2)}) copy-start(f32[320]{0:T(512)} %param.33) | copy-start | bytes 3844
  125.3 200.8 %copy-start.3 = (bf16[320,320]{1,0:T(8,128)(2,1)S(1)}, bf16[320,320]{1,0:T(8,128)(2,1)}, u32[]{:S(2)}) copy-start(bf16[320,320]{1,0:T(8,128)(2,1)} %param.34) | copy-start | bytes 614404
  125.3 200.8 %copy-start.13 = (f32[320]{0:T(512)S(1)}, f32[320]{0:T(512)}, u32[]{:S(2)}) copy-start(f32[320]{0:T(512)} %param.35) | copy-start | bytes 3844
  324.7 1.9 copy-start.17
  324.7 1.9 copy-start.19
  324.7 1.9 copy-start.20
  326.7 20.2 %copy-start.6 = (f32[9,1280]{1,0:T(8,128)S(1)}, f32[9,1280]{1,0:T(8,128)}, u32[]{:S(2)}) copy-start(f32[9,1280]{1,0:T(8,128)} %param.40) | copy-start | bytes 138244
  327.7 7.0 %collective-permute-start.1 = (bf16[1,16,1280]{2,1,0:T(8,128)(2,1)S(1)}, bf16[1,16,1280]{2,1,0:T(8,128)(2,1)S(1)}, u32[]{:S(2)}, u32[]{:S(2)}) collective-permute-start(bf16[1,16,1280]{2,1,0:T(8,128)(2,1)S(1)} %get-tuple-element.19), channel_id=1, source_target_pairs={{16,0},{32,16},{48,32},{64,48},{80,64},{96,80},{112,96},{17,1},{33... | collective-permute-start | bytes 122888 | tf_op jit(solution)/shard_map/ppermute | solution.py:19
  331.8 7.1 %collective-permute-start = (bf16[1,16,1280]{2,1,0:T(8,128)(2,1)S(1)}, bf16[1,16,1280]{2,1,0:T(8,128)(2,1)S(1)}, u32[]{:S(2)}, u32[]{:S(2)}) collective-permute-start(bf16[1,16,1280]{2,1,0:T(8,128)(2,1)S(1)} %get-tuple-element.18), channel_id=1, source_target_pairs={{0,16},{16,32},{32,48},{48,64},{64,80},{80,96},{96,112},{1,17},{17... | collective-permute-start | bytes 122888 | tf_op jit(solution)/shard_map/ppermute | solution.py:18
  339.2 8.1 %collective-permute-start.2 = (bf16[34,1,1280]{2,1,0:T(2,128)(2,1)S(1)}, bf16[34,1,1280]{2,1,0:T(2,128)(2,1)S(1)}, u32[]{:S(2)}, u32[]{:S(2)}) collective-permute-start(bf16[34,1,1280]{2,1,0:T(2,128)(2,1)S(1)} %get-tuple-element.16), channel_id=1, source_target_pairs={{0,1},{1,2},{2,3},{3,4},{4,5},{5,6},{6,7},{7,8},{8,9},{9,10},{10,1... | collective-permute-start | bytes 261128 | tf_op jit(solution)/shard_map/ppermute | solution.py:18
  345.0 7.6 %collective-permute-start.3 = (bf16[34,1,1280]{2,1,0:T(2,128)(2,1)S(1)}, bf16[34,1,1280]{2,1,0:T(2,128)(2,1)S(1)}, u32[]{:S(2)}, u32[]{:S(2)}) collective-permute-start(bf16[34,1,1280]{2,1,0:T(2,128)(2,1)S(1)} %get-tuple-element.17), channel_id=1, source_target_pairs={{1,0},{2,1},{3,2},{4,3},{5,4},{6,5},{7,6},{8,7},{9,8},{10,9},{11,1... | collective-permute-start | bytes 261128 | tf_op jit(solution)/shard_map/ppermute | solution.py:19
  347.0 6.8 %copy-start.7 = (f32[1280]{0:T(1024)S(1)}, f32[1280]{0:T(1024)}, u32[]{:S(2)}) copy-start(f32[1280]{0:T(1024)} %param.41) | copy-start | bytes 15364
  353.9 9.0 %copy-start.15 = (bf16[1280,320]{0,1:T(8,128)(2,1)S(1)}, bf16[1280,320]{0,1:T(8,128)(2,1)}, u32[]{:S(2)}) copy-start(bf16[1280,320]{0,1:T(8,128)(2,1)} %param.42) | copy-start | bytes 2457604
  353.9 9.0 %copy-start.21 = (f32[320]{0:T(512)S(1)}, f32[320]{0:T(512)}, u32[]{:S(2)}) copy-start(f32[320]{0:T(512)} %param.43) | copy-start | bytes 3844
Sparse Core Ops, SparseCore 0:
  44.1 81.1 all-gather.1

commit v3 on v2

--- a/solution.py
+++ b/solution.py
@@ -28,64 +28,79 @@
     return centered * lax.rsqrt(var + 1e-06) * gain + shift
 
 
-KV_BLOCK = 512
-
-
-def attend_kernel(q_ref, rn_ref, wk_ref, wv_ref, bv_ref, o_ref, m_ref, l_ref, acc_ref):
+KV_BLOCK = 4096
+LANES = 128
+
+
+def attend_kernel(q_ref, rn_ref, w_ref, b_ref, o_ref, m_ref, acc_ref):
     step = pl.program_id(0)
+    heads, count, head_dim = o_ref.shape
 
     @pl.when(step == 0)
     def _():
         m_ref[...] = jnp.full(m_ref.shape, -1e30, jnp.float32)
-        l_ref[...] = jnp.zeros(l_ref.shape, jnp.float32)
         acc_ref[...] = jnp.zeros(acc_ref.shape, jnp.float32)
 
-    rn = rn_ref[...]
-    for h in range(HEADS):
-        k_h = jnp.dot(rn, wk_ref[h], preferred_element_type=jnp.float32).astype(jnp.bfloat16)
-        v_h = (jnp.dot(rn, wv_ref[h], preferred_element_type=jnp.float32) + bv_ref[h]).astype(
-            jnp.bfloat16
-        )
+    projected = (
+        jnp.dot(rn_ref[...], w_ref[...], preferred_element_type=jnp.float32) + b_ref[...]
+    ).astype(jnp.bfloat16)
+    for h in range(heads):
+        k_h = projected[:, h * LANES : (h + 1) * LANES]
+        v_h = projected[:, (heads + h) * LANES : (heads + h + 1) * LANES]
         scores = lax.dot_general(
             q_ref[h], k_h, (((1,), (1,)), ((), ())), preferred_element_type=jnp.float32
         )
         run_max = m_ref[h]
         new_max = jnp.maximum(run_max, jnp.max(scores, axis=-1, keepdims=True))
         factor = jnp.exp(run_max - new_max)
-        expo = jnp.exp(scores - new_max)
-        l_ref[h] = l_ref[h] * factor + jnp.sum(expo, axis=-1, keepdims=True)
-        acc_ref[h] = acc_ref[h] * factor + jnp.dot(
-            expo.astype(jnp.bfloat16), v_h, preferred_element_type=jnp.float32
-        )
+        expo = jnp.exp(scores - new_max).astype(jnp.bfloat16)
+        acc_ref[h] = acc_ref[h] * factor + jnp.dot(expo, v_h, preferred_element_type=jnp.float32)
         m_ref[h] = new_max
 
     @pl.when(step == pl.num_programs(0) - 1)
     def _():
-        o_ref[...] = (acc_ref[...] / l_ref[...]).astype(o_ref.dtype)
-
-
-def attend(query_heads, gathered, wk_heads, wv_heads, bv_heads):
-    heads, count, head_dim = query_heads.shape
-    length, chans = gathered.shape
-    return pl.pallas_call(
+        acc = acc_ref[...]
+        o_ref[...] = (acc[:, :, :head_dim] / acc[:, :, head_dim : head_dim + 1]).astype(o_ref.dtype)
+
+
+def attend(query, gathered, w_key, w_value, b_value):
+    count, chans = query.shape
+    length = gathered.shape[0]
+    head_dim = chans // HEADS
+    spare = LANES - head_dim
+
+    def by_head(w):
+        w = w.reshape(chans, HEADS, head_dim)
+        return jnp.pad(w, ((0, 0), (0, 0), (0, spare))).reshape(chans, HEADS * LANES)
+
+    weights = jnp.concatenate([by_head(w_key), by_head(w_value)], axis=1)
+    value_bias = jnp.pad(b_value.reshape(HEADS, head_dim), ((0, 0), (0, spare)))
+    value_bias = value_bias.at[:, head_dim].set(1.0)
+    bias = jnp.concatenate([jnp.zeros((HEADS * LANES,), jnp.float32), value_bias.reshape(-1)])
+    bias = bias.reshape(1, -1)
+    query_heads = jnp.pad(
+        query.reshape(count, HEADS, head_dim).transpose(1, 0, 2), ((0, 0), (0, 0), (0, spare))
+    )
+    out = pl.pallas_call(
         attend_kernel,
         grid=(length // KV_BLOCK,),
         in_specs=[
-            pl.BlockSpec((heads, count, head_dim), lambda j: (0, 0, 0)),
+            pl.BlockSpec((HEADS, count, LANES), lambda j: (0, 0, 0)),
             pl.BlockSpec((KV_BLOCK, chans), lambda j: (j, 0)),
-            pl.BlockSpec((heads, chans, head_dim), lambda j: (0, 0, 0)),
-            pl.BlockSpec((heads, chans, head_dim), lambda j: (0, 0, 0)),
-            pl.BlockSpec((heads, 1, head_dim), lambda j: (0, 0, 0)),
+            pl.BlockSpec(weights.shape, lambda j: (0, 0)),
+            pl.BlockSpec(bias.shape, lambda j: (0, 0)),
         ],
-        out_specs=pl.BlockSpec((heads, count, head_dim), lambda j: (0, 0, 0)),
-        out_shape=jax.ShapeDtypeStruct((heads, count, head_dim), jnp.bfloat16),
+        out_specs=pl.BlockSpec((HEADS, count, head_dim), lambda j: (0, 0, 0)),
+        out_shape=jax.ShapeDtypeStruct((HEADS, count, head_dim), jnp.bfloat16),
         scratch_shapes=[
-            pltpu.VMEM((heads, count, 1), jnp.float32),
-            pltpu.VMEM((heads, count, 1), jnp.float32),
-            pltpu.VMEM((heads, count, head_dim), jnp.float32),
+            pltpu.VMEM((HEADS, count, 1), jnp.float32),
+            pltpu.VMEM((HEADS, count, LANES), jnp.float32),
         ],
-        compiler_params=pltpu.CompilerParams(dimension_semantics=("arbitrary",)),
-    )(query_heads, gathered, wk_heads, wv_heads, bv_heads)
+        compiler_params=pltpu.CompilerParams(
+            dimension_semantics=("arbitrary",), vmem_limit_bytes=60 * 1024 * 1024
+        ),
+    )(query_heads, gathered, weights, bias)
+    return out.transpose(1, 0, 2).reshape(count, chans)
 
 
 def per_device(
@@ -121,7 +136,6 @@
         (jnp.dot(normed, w_query, preferred_element_type=jnp.float32) + b_query)
         * head_dim ** (-0.5)
     ).astype(jnp.bfloat16)
-    query = query.reshape(count, HEADS, head_dim)
     blocks = (
         normed.reshape(tile_r // 2, 2, tile_c // 2, 2, chans)
         .transpose(0, 2, 1, 3, 4)
@@ -132,11 +146,7 @@
 
     gathered = lax.all_gather(reduced_norm, "rows", axis=0, tiled=True)
     gathered = lax.all_gather(gathered, "cols", axis=0, tiled=True)
-    wk_heads = w_key.reshape(chans, HEADS, head_dim).transpose(1, 0, 2)
-    wv_heads = w_value.reshape(chans, HEADS, head_dim).transpose(1, 0, 2)
-    bv_heads = b_value.reshape(HEADS, 1, head_dim)
-    attended = attend(query.transpose(1, 0, 2), gathered, wk_heads, wv_heads, bv_heads)
-    attended = attended.transpose(1, 0, 2).reshape(count, chans)
+    attended = attend(query, gathered, w_key, w_value, b_value)
     mid = (flat + jnp.dot(attended, w_out, preferred_element_type=jnp.float32) + b_out).astype(
         jnp.bfloat16
     )

time: 372 us -> 256 us (0.69)
  Pallas kernels: 199 us -> 84.5 us
  waiting for transfers between devices: 86 us -> 81.8 us
    pallas_call x1, Pallas kernels: 199 us -> 84.5 us  [attend(): pl.pallas_call(attend_kernel, grid=(length // KV_BLOCK,), in_specs=[pl.Bl...]
    ppermute x2, waiting for transfers between devices: 4.48 us -> 0.27 us  [padded_2(): before = lax.ppermute(last, axis, up)]
  transfers between devices with their start and end apart: 5 -> 5, of which waited for: 4 -> 4; matrix products, arithmetic and copies ran while one was open for 1% -> 3% of each run, Pallas kernels for 0% -> 0%
where the time goes in v3:
time: 256 us; the launch traced here: 255 us
  Pallas kernels  84.5 us (33%)
  waiting for transfers between devices  81.8 us (32%)
  blocking collectives  30.8 us (12%)
  starting transfers between devices  15.4 us (6%)
  other arithmetic  15.4 us (6%)
  between operations  14.6 us (6%)
  local copies, waits for them, and re-layouts  8.7 us (3%)
  matrix products  4.05 us (2%)
    pallas_call x1, Pallas kernels, attend(): pl.pallas_call(attend_kernel, grid=(length // KV_BLOCK,), in_specs=[pl.Bl...  84.5 us
    all_gather x1, waiting for transfers between devices, per_device(): gathered = lax.all_gather(gathered, 'cols', axis=0, tiled=True)  73.9 us
    all_gather x1, blocking collectives, per_device(): gathered = lax.all_gather(reduced_norm, 'rows', axis=0, tiled=True)  30.8 us
    ppermute x2, starting transfers between devices, padded_2(): before = lax.ppermute(last, axis, up)  9.51 us
    convert_element_type x1, other arithmetic, per_device(): jax.nn.gelu(spread, approximate=False).astype(jnp.bfloat16)  9 us
    ppermute x2, waiting for transfers between devices, padded_2(): after = lax.ppermute(initial, axis, down)  7.58 us
    ppermute x2, starting transfers between devices, padded_2(): after = lax.ppermute(initial, axis, down)  5.87 us
  transfers between devices with their start and end apart: 5, of which 4 were waited for; matrix products, arithmetic and copies ran while one was open for 3% of the time, Pallas kernels for 0%

profile of v3, /device:TPU:15, one launch (start us, length us, event | category | flops | bytes accessed | tf_op | source)
XLA Modules:
  0.0 255.2 jit_solution(14041753254733890381)
XLA Ops:
  6.5 1.2 convert_reduce_fusion
  7.8 0.0 copy-start.2
  7.8 0.0 copy-start.8
  7.8 1.3 multiply_reduce_fusion
  9.1 0.1 reshape.189
  9.2 1.4 reshape.188
  10.6 0.0 copy-start.9
  10.7 0.0 copy-start.10
  10.7 0.1 reshape.190
  10.8 0.3 copy.74
  11.0 0.3 copy.71
  11.3 0.2 fusion.22
  11.6 0.0 copy-start.1
  11.6 0.3 copy.75
  11.9 0.0 copy-start.14
  11.9 0.0 copy-start.4
  11.9 0.3 reshape.175
  12.2 0.5 fusion.31
  12.8 0.2 multiply_reduce_fusion.2
  13.0 0.0 copy-start.5
  13.0 0.1 add_convert_fusion.4
  13.1 30.8 %all_gather.6 = bf16[1024,320]{1,0:T(8,128)(2,1)} all-gather(bf16[128,320]{1,0:T(8,128)(2,1)S(1)} %add_convert_fusion.4), channel_id=1, replica_groups=mesh['rows'=8,'cols'=16] {'rows'}, dimensions={0}, use_global_device_ids=true | all-gather | bytes 737280 | tf_op jit(solution)/shard_map/all_gather | solution.py:147
  43.9 0.0 all-gather.2.cloned.1.call-update
  43.9 0.1 div.23
  44.0 0.1 rsqrt.32
  44.1 0.1 convert_element_type.105
  44.2 0.1 reshape.180
  44.3 0.6 compare_reduce_fusion
  45.6 0.1 scatter.4
  45.7 0.6 reshape.182.b_ref
  46.3 0.2 copy.77
  46.5 0.0 copy-start.17
  46.6 0.2 copy.79
  46.8 0.2 copy.78
  47.1 0.2 copy.80
  47.3 0.2 copy.82
  47.6 1.5 fusion.14
  49.1 0.3 copy.69
  49.4 1.0 pad.18.q_ref
  50.4 1.0 pad_maximum_fusion.3.w_ref
  51.4 73.9 %all-gather.2.cloned.1.call-done.rn_ref = bf16[16384,320]{1,0:T(8,128)(2,1)} async-done(((bf16[1024,320]{1,0:T(8,128)(2,1)}), bf16[16384,320]{1,0:T(8,128)(2,1)}) %all-gather.2.cloned.1.call-update) | async-done | bytes 10485776 | tf_op jit(solution)/shard_map/all_gather | solution.py:148
  125.3 84.5 %shard_map.208 = bf16[5,512,64]{2,1,0:T(8,128)(2,1)} custom-call(bf16[5,512,128]{2,1,0:T(8,128)(2,1)} %pad.18.q_ref, bf16[16384,320]{1,0:T(8,128)(2,1)} %all-gather.2.cloned.1.call-done.rn_ref, bf16[320,1280]{1,0:T(8,128)(2,1)} %pad_maximum_fusion.3.w_ref, f32[1,1280]{1,0:T(1,128)} %reshape.182.b_ref), custom_call_target="tpu_custom_call" | custom-call | tf_op jit(solution)/shard_map/pallas_call | solution.py:84
  209.8 1.3 copy.81
  211.2 0.4 fusion.32
  211.6 0.1 multiply_reduce_fusion.1
  211.8 0.0 copy-start.6
  211.8 1.0 fusion
  212.8 3.7 %collective-permute-start = (bf16[1,16,1280]{2,1,0:T(8,128)(2,1)S(1)}, bf16[1,16,1280]{2,1,0:T(8,128)(2,1)S(1)}, u32[]{:S(2)}, u32[]{:S(2)}) collective-permute-start(bf16[1,16,1280]{2,1,0:T(8,128)(2,1)S(1)} %get-tuple-element.30), channel_id=1, source_target_pairs={{0,16},{16,32},{32,48},{48,64},{64,80},{80,96},{96,112},{1,17},{17... | collective-permute-start | bytes 122888 | tf_op jit(solution)/shard_map/ppermute | solution.py:18
  216.6 3.9 %collective-permute-start.1 = (bf16[1,16,1280]{2,1,0:T(8,128)(2,1)S(1)}, bf16[1,16,1280]{2,1,0:T(8,128)(2,1)S(1)}, u32[]{:S(2)}, u32[]{:S(2)}) collective-permute-start(bf16[1,16,1280]{2,1,0:T(8,128)(2,1)S(1)} %get-tuple-element.31), channel_id=1, source_target_pairs={{16,0},{32,16},{48,32},{64,48},{80,64},{96,80},{112,96},{17,1},{33... | collective-permute-start | bytes 122888 | tf_op jit(solution)/shard_map/ppermute | solution.py:19
  220.5 0.0 collective-permute-done
  220.5 2.3 collective-permute-done.1
  222.8 0.3 pad_maximum_fusion.6
  223.1 5.8 %collective-permute-start.2 = (bf16[34,1,1280]{2,1,0:T(2,128)(2,1)S(1)}, bf16[34,1,1280]{2,1,0:T(2,128)(2,1)S(1)}, u32[]{:S(2)}, u32[]{:S(2)}) collective-permute-start(bf16[34,1,1280]{2,1,0:T(2,128)(2,1)S(1)} %get-tuple-element.28), channel_id=1, source_target_pairs={{0,1},{1,2},{2,3},{3,4},{4,5},{5,6},{6,7},{7,8},{8,9},{9,10},{10,1... | collective-permute-start | bytes 261128 | tf_op jit(solution)/shard_map/ppermute | solution.py:18
  228.9 1.9 collective-permute-start.3
  230.8 0.1 slice_reduce_fusion.8
  230.9 0.0 copy-start.7
  231.0 0.3 collective-permute-done.2
  231.2 5.3 %collective-permute-done.3 = bf16[34,1,1280]{2,1,0:T(2,128)(2,1)S(1)} collective-permute-done((bf16[34,1,1280]{2,1,0:T(2,128)(2,1)S(1)}, bf16[34,1,1280]{2,1,0:T(2,128)(2,1)S(1)}, u32[]{:S(2)}, u32[]{:S(2)}) %collective-permute-start.3) | collective-permute-done | bytes 87072 | tf_op jit(solution)/shard_map/ppermute | solution.py:19
  236.5 1.3 maximum_maximum_fusion
  237.8 0.0 copy-start.15
  237.8 0.0 copy-start.20
  237.8 9.0 %fusion.3 = bf16[32,16,1280]{2,1,0:T(8,128)(2,1)S(1)} fusion(bf16[32,16,1280]{2,1,0:T(8,128)(2,1)S(1)} %bitcast.29, bf16[34,17,1280]{2,1,0:T(8,128)(2,1)S(1)} %get-tuple-element.27, bf16[1,16,1280]{2,1,0:T(8,128)(2,1)S(1)} %collective-permute-done.1, bf16[34,17,1280]{2,1,0:T(8,128)(2,1)S(1)} %get-tuple-element.26, ...), kind=kLoop, calls=%fused_computation.5 | loop fusion | flops 61603840 | bytes 10618880 | tf_op jit(solution)/shard_map/convert_element_type | solution.py:167
  246.8 0.6 fusion.17
  247.5 0.9 copy.83
  (42 shorter events, 0.2 us)
Async XLA Ops:
  6.5 205.2 %copy-start = (bf16[320,1280]{1,0:T(8,128)(2,1)S(1)}, bf16[320,1280]{1,0:T(8,128)(2,1)}, u32[]{:S(2)}) copy-start(bf16[320,1280]{1,0:T(8,128)(2,1)} %param.40) | copy-start | bytes 2457604
  6.5 4.8 %copy-start.11 = (f32[320]{0:T(512)S(1)}, f32[320]{0:T(512)}, u32[]{:S(2)}) copy-start(f32[320]{0:T(512)} %param.26) | copy-start | bytes 3844
  6.5 4.8 %copy-start.12 = (f32[320]{0:T(512)S(1)}, f32[320]{0:T(512)}, u32[]{:S(2)}) copy-start(f32[320]{0:T(512)} %param.25) | copy-start | bytes 3844
  6.5 118.8 %all-gather.2.cloned.1.call-start = ((), (), s32[]{:S(2)}) async-start(), calls=%async_computation | async-start | bytes 13369344 | tf_op jit(solution)/shard_map/all_gather | solution.py:148
  7.8 4.5 %copy-start.2 = (bf16[1280,320]{0,1:T(8,128)(2,1)S(1)}, bf16[1280,320]{0,1:T(8,128)(2,1)}, u32[]{:S(2)}) copy-start(bf16[1280,320]{0,1:T(8,128)(2,1)} %param.29) | copy-start | bytes 2457604
  7.8 4.5 %copy-start.8 = (f32[320]{0:T(512)S(1)}, f32[320]{0:T(512)}, u32[]{:S(2)}) copy-start(f32[320]{0:T(512)} %param.30) | copy-start | bytes 3844
  10.6 2.3 copy-start.9
  10.7 2.3 copy-start.10
  11.6 32.6 %copy-start.1 = (bf16[32,16,320]{2,1,0:T(8,128)(2,1)S(1)}, bf16[32,16,320]{2,1,0:T(8,128)(2,1)}, u32[]{:S(2)}) copy-start(bf16[32,16,320]{2,1,0:T(8,128)(2,1)} %param.24) | copy-start | bytes 983044
  11.9 32.3 %copy-start.14 = (f32[320]{0:T(512)S(1)}, f32[320]{0:T(512)}, u32[]{:S(2)}) copy-start(f32[320]{0:T(512)} %param.35) | copy-start | bytes 3844
  11.9 34.4 %copy-start.4 = (bf16[320,320]{1,0:T(8,128)(2,1)S(1)}, bf16[320,320]{1,0:T(8,128)(2,1)}, u32[]{:S(2)}) copy-start(bf16[320,320]{1,0:T(8,128)(2,1)} %param.33) | copy-start | bytes 614404
  13.0 33.8 %copy-start.5 = (bf16[320,320]{1,0:T(8,128)(2,1)S(1)}, bf16[320,320]{1,0:T(8,128)(2,1)}, u32[]{:S(2)}) copy-start(bf16[320,320]{1,0:T(8,128)(2,1)} %param.34) | copy-start | bytes 614404
  46.5 1.1 copy-start.17
  51.4 159.8 %copy-start.3 = (bf16[320,320]{1,0:T(8,128)(2,1)S(1)}, bf16[320,320]{1,0:T(8,128)(2,1)}, u32[]{:S(2)}) copy-start(bf16[320,320]{1,0:T(8,128)(2,1)} %param.36) | copy-start | bytes 614404
  51.4 159.8 %copy-start.13 = (f32[320]{0:T(512)S(1)}, f32[320]{0:T(512)}, u32[]{:S(2)}) copy-start(f32[320]{0:T(512)} %param.37) | copy-start | bytes 3844
  209.8 1.9 copy-start.16
  209.8 1.9 copy-start.18
  209.8 1.9 copy-start.19
  211.8 19.0 %copy-start.6 = (f32[9,1280]{1,0:T(8,128)S(1)}, f32[9,1280]{1,0:T(8,128)}, u32[]{:S(2)}) copy-start(f32[9,1280]{1,0:T(8,128)} %param.42) | copy-start | bytes 138244
  212.8 7.7 %collective-permute-start = (bf16[1,16,1280]{2,1,0:T(8,128)(2,1)S(1)}, bf16[1,16,1280]{2,1,0:T(8,128)(2,1)S(1)}, u32[]{:S(2)}, u32[]{:S(2)}) collective-permute-start(bf16[1,16,1280]{2,1,0:T(8,128)(2,1)S(1)} %get-tuple-element.30), channel_id=1, source_target_pairs={{0,16},{16,32},{32,48},{48,64},{64,80},{80,96},{96,112},{1,17},{17... | collective-permute-start | bytes 122888 | tf_op jit(solution)/shard_map/ppermute | solution.py:18
  216.6 6.3 %collective-permute-start.1 = (bf16[1,16,1280]{2,1,0:T(8,128)(2,1)S(1)}, bf16[1,16,1280]{2,1,0:T(8,128)(2,1)S(1)}, u32[]{:S(2)}, u32[]{:S(2)}) collective-permute-start(bf16[1,16,1280]{2,1,0:T(8,128)(2,1)S(1)} %get-tuple-element.31), channel_id=1, source_target_pairs={{16,0},{32,16},{48,32},{64,48},{80,64},{96,80},{112,96},{17,1},{33... | collective-permute-start | bytes 122888 | tf_op jit(solution)/shard_map/ppermute | solution.py:19
  223.1 8.1 %collective-permute-start.2 = (bf16[34,1,1280]{2,1,0:T(2,128)(2,1)S(1)}, bf16[34,1,1280]{2,1,0:T(2,128)(2,1)S(1)}, u32[]{:S(2)}, u32[]{:S(2)}) collective-permute-start(bf16[34,1,1280]{2,1,0:T(2,128)(2,1)S(1)} %get-tuple-element.28), channel_id=1, source_target_pairs={{0,1},{1,2},{2,3},{3,4},{4,5},{5,6},{6,7},{7,8},{8,9},{9,10},{10,1... | collective-permute-start | bytes 261128 | tf_op jit(solution)/shard_map/ppermute | solution.py:18
  228.9 7.6 %collective-permute-start.3 = (bf16[34,1,1280]{2,1,0:T(2,128)(2,1)S(1)}, bf16[34,1,1280]{2,1,0:T(2,128)(2,1)S(1)}, u32[]{:S(2)}, u32[]{:S(2)}) collective-permute-start(bf16[34,1,1280]{2,1,0:T(2,128)(2,1)S(1)} %get-tuple-element.29), channel_id=1, source_target_pairs={{1,0},{2,1},{3,2},{4,3},{5,4},{6,5},{7,6},{8,7},{9,8},{10,9},{11,1... | collective-permute-start | bytes 261128 | tf_op jit(solution)/shard_map/ppermute | solution.py:19
  230.9 6.8 %copy-start.7 = (f32[1280]{0:T(1024)S(1)}, f32[1280]{0:T(1024)}, u32[]{:S(2)}) copy-start(f32[1280]{0:T(1024)} %param.43) | copy-start | bytes 15364
  237.8 9.0 %copy-start.15 = (bf16[1280,320]{0,1:T(8,128)(2,1)S(1)}, bf16[1280,320]{0,1:T(8,128)(2,1)}, u32[]{:S(2)}) copy-start(bf16[1280,320]{0,1:T(8,128)(2,1)} %param.44) | copy-start | bytes 2457604
  237.8 9.0 %copy-start.20 = (f32[320]{0:T(512)S(1)}, f32[320]{0:T(512)}, u32[]{:S(2)}) copy-start(f32[320]{0:T(512)} %param.45) | copy-start | bytes 3844
Sparse Core Ops, SparseCore 0:
  44.1 81.1 all-gather.1

commit v4 on v3

--- a/solution.py
+++ b/solution.py
@@ -21,6 +21,15 @@
     return value
 
 
+def gather_rows(value, axis):
+    devices = lax.axis_size(axis)
+    pieces = [value]
+    for shift in range(1, devices):
+        pairs = [(i, (i + shift) % devices) for i in range(devices)]
+        pieces.append(lax.ppermute(value, axis, pairs))
+    return jnp.concatenate(pieces, axis=0)
+
+
 def layer_norm(value, gain, shift):
     mean = jnp.mean(value, axis=-1, keepdims=True)
     centered = value - mean
@@ -32,21 +41,23 @@
 LANES = 128
 
 
-def attend_kernel(q_ref, rn_ref, w_ref, b_ref, o_ref, m_ref, acc_ref):
+def attend_kernel(q_ref, rn_ref, w_ref, b_ref, m_in_ref, acc_in_ref, m_ref, acc_ref):
     step = pl.program_id(0)
-    heads, count, head_dim = o_ref.shape
+    heads = q_ref.shape[0]
 
     @pl.when(step == 0)
     def _():
-        m_ref[...] = jnp.full(m_ref.shape, -1e30, jnp.float32)
-        acc_ref[...] = jnp.zeros(acc_ref.shape, jnp.float32)
-
-    projected = (
-        jnp.dot(rn_ref[...], w_ref[...], preferred_element_type=jnp.float32) + b_ref[...]
-    ).astype(jnp.bfloat16)
-    for h in range(heads):
-        k_h = projected[:, h * LANES : (h + 1) * LANES]
-        v_h = projected[:, (heads + h) * LANES : (heads + h + 1) * LANES]
+        m_ref[...] = m_in_ref[...]
+        acc_ref[...] = acc_in_ref[...]
+
+    rn = rn_ref[...]
+
+    def one_head(h, carry):
+        projected = (
+            jnp.dot(rn, w_ref[h], preferred_element_type=jnp.float32) + b_ref[h]
+        ).astype(jnp.bfloat16)
+        k_h = projected[:, :LANES]
+        v_h = projected[:, LANES:]
         scores = lax.dot_general(
             q_ref[h], k_h, (((1,), (1,)), ((), ())), preferred_element_type=jnp.float32
         )
@@ -56,50 +67,60 @@
         expo = jnp.exp(scores - new_max).astype(jnp.bfloat16)
         acc_ref[h] = acc_ref[h] * factor + jnp.dot(expo, v_h, preferred_element_type=jnp.float32)
         m_ref[h] = new_max
-
-    @pl.when(step == pl.num_programs(0) - 1)
-    def _():
-        acc = acc_ref[...]
-        o_ref[...] = (acc[:, :, :head_dim] / acc[:, :, head_dim : head_dim + 1]).astype(o_ref.dtype)
-
-
-def attend(query, gathered, w_key, w_value, b_value):
-    count, chans = query.shape
-    length = gathered.shape[0]
-    head_dim = chans // HEADS
-    spare = LANES - head_dim
-
-    def by_head(w):
-        w = w.reshape(chans, HEADS, head_dim)
-        return jnp.pad(w, ((0, 0), (0, 0), (0, spare))).reshape(chans, HEADS * LANES)
-
-    weights = jnp.concatenate([by_head(w_key), by_head(w_value)], axis=1)
-    value_bias = jnp.pad(b_value.reshape(HEADS, head_dim), ((0, 0), (0, spare)))
-    value_bias = value_bias.at[:, head_dim].set(1.0)
-    bias = jnp.concatenate([jnp.zeros((HEADS * LANES,), jnp.float32), value_bias.reshape(-1)])
-    bias = bias.reshape(1, -1)
-    query_heads = jnp.pad(
-        query.reshape(count, HEADS, head_dim).transpose(1, 0, 2), ((0, 0), (0, 0), (0, spare))
-    )
-    out = pl.pallas_call(
+        return carry
+
+    lax.fori_loop(0, heads, one_head, 0)
+
+
+def attend_part(query_heads, part, weights, bias, run_max, accum):
+    heads, count, lanes = query_heads.shape
+    length, chans = part.shape
+    state = pl.BlockSpec((heads, count, 1), lambda j: (0, 0, 0))
+    whole = pl.BlockSpec((heads, count, lanes), lambda j: (0, 0, 0))
+    return pl.pallas_call(
         attend_kernel,
         grid=(length // KV_BLOCK,),
         in_specs=[
-            pl.BlockSpec((HEADS, count, LANES), lambda j: (0, 0, 0)),
+            whole,
             pl.BlockSpec((KV_BLOCK, chans), lambda j: (j, 0)),
-            pl.BlockSpec(weights.shape, lambda j: (0, 0)),
-            pl.BlockSpec(bias.shape, lambda j: (0, 0)),
+            pl.BlockSpec(weights.shape, lambda j: (0, 0, 0)),
+            pl.BlockSpec(bias.shape, lambda j: (0, 0, 0)),
+            state,
+            whole,
         ],
-        out_specs=pl.BlockSpec((HEADS, count, head_dim), lambda j: (0, 0, 0)),
-        out_shape=jax.ShapeDtypeStruct((HEADS, count, head_dim), jnp.bfloat16),
-        scratch_shapes=[
-            pltpu.VMEM((HEADS, count, 1), jnp.float32),
-            pltpu.VMEM((HEADS, count, LANES), jnp.float32),
+        out_specs=[state, whole],
+        out_shape=[
+            jax.ShapeDtypeStruct(run_max.shape, jnp.float32),
+            jax.ShapeDtypeStruct(accum.shape, jnp.float32),
         ],
         compiler_params=pltpu.CompilerParams(
             dimension_semantics=("arbitrary",), vmem_limit_bytes=60 * 1024 * 1024
         ),
-    )(query_heads, gathered, weights, bias)
+    )(query_heads, part, weights, bias, run_max, accum)
+
+
+def attend(query, parts, w_key, w_value, b_value):
+    count, chans = query.shape
+    head_dim = chans // HEADS
+    spare = LANES - head_dim
+
+    def by_head(w):
+        w = w.reshape(chans, HEADS, head_dim).transpose(1, 0, 2)
+        return jnp.pad(w, ((0, 0), (0, 0), (0, spare)))
+
+    weights = jnp.concatenate([by_head(w_key), by_head(w_value)], axis=2)
+    value_bias = jnp.pad(b_value.reshape(HEADS, head_dim), ((0, 0), (0, spare)))
+    value_bias = value_bias.at[:, head_dim].set(1.0)
+    bias = jnp.concatenate([jnp.zeros((HEADS, LANES), jnp.float32), value_bias], axis=1)
+    bias = bias.reshape(HEADS, 1, 2 * LANES)
+    query_heads = jnp.pad(
+        query.reshape(count, HEADS, head_dim).transpose(1, 0, 2), ((0, 0), (0, 0), (0, spare))
+    )
+    run_max = jnp.full((HEADS, count, 1), -1e30, jnp.float32)
+    accum = jnp.zeros((HEADS, count, LANES), jnp.float32)
+    for part in parts:
+        run_max, accum = attend_part(query_heads, part, weights, bias, run_max, accum)
+    out = (accum[:, :, :head_dim] / accum[:, :, head_dim : head_dim + 1]).astype(jnp.bfloat16)
     return out.transpose(1, 0, 2).reshape(count, chans)
 
 
@@ -144,9 +165,13 @@
     reduced = jnp.dot(blocks, w_reduce, preferred_element_type=jnp.float32) + b_reduce
     reduced_norm = layer_norm(reduced, reduce_gain, reduce_shift).astype(jnp.bfloat16)
 
-    gathered = lax.all_gather(reduced_norm, "rows", axis=0, tiled=True)
-    gathered = lax.all_gather(gathered, "cols", axis=0, tiled=True)
-    attended = attend(query, gathered, w_key, w_value, b_value)
+    gathered = gather_rows(reduced_norm, "rows")
+    half = gathered.shape[0] // 2
+    parts = [
+        lax.all_gather(gathered[:half], "cols", axis=0, tiled=True),
+        lax.all_gather(gathered[half:], "cols", axis=0, tiled=True),
+    ]
+    attended = attend(query, parts, w_key, w_value, b_value)
     mid = (flat + jnp.dot(attended, w_out, preferred_element_type=jnp.float32) + b_out).astype(
         jnp.bfloat16
     )

time: 256 us -> 238 us (0.930)
  waiting for transfers between devices: 81.8 us -> 39.3 us
  Pallas kernels: 84.5 us -> 120 us
  blocking collectives: 30.8 us -> 0 us
  starting transfers between devices: 15.4 us -> 27.4 us
  other arithmetic: 15.4 us -> 18.9 us
  local copies, waits for them, and re-layouts: 8.7 us -> 12.1 us
    all_gather x1 -> x2, waiting for transfers between devices: 73.9 us -> 26.9 us  [the longest x1 26.9 us: per_device(): lax.all_gather(gathered[:half], 'cols', axis=0, tiled=True)]
    pallas_call x1 -> x2, Pallas kernels: 84.5 us -> 120 us  [attend_part(): pl.pallas_call(attend_kernel, grid=(length // KV_BLOCK,), in_specs=[whole...]
    all_gather x1 -> x0, blocking collectives: 30.8 us -> none  [per_device(): gathered = lax.all_gather(reduced_norm, 'rows', axis=0, tiled=True)]
    ppermute x0 -> x7, starting transfers between devices: none -> 12.1 us  [gather_rows(): pieces.append(lax.ppermute(value, axis, pairs))]
    ppermute x0 -> x7, waiting for transfers between devices: none -> 8.2 us  [gather_rows(): pieces.append(lax.ppermute(value, axis, pairs))]
    ppermute x2, waiting for transfers between devices: 7.58 us -> 3.02 us  [padded_2(): after = lax.ppermute(initial, axis, down)]
  transfers between devices with their start and end apart: 5 -> 13, of which waited for: 4 -> 8; matrix products, arithmetic and copies ran while one was open for 3% -> 4% of each run, Pallas kernels for 0% -> 25%
where the time goes in v4:
time: 238 us; the launch traced here: 237 us
  Pallas kernels  120 us (50%)
  waiting for transfers between devices  39.3 us (17%)
  starting transfers between devices  27.4 us (12%)
  other arithmetic  18.9 us (8%)
  between operations  14.6 us (6%)
  local copies, waits for them, and re-layouts  12.1 us (5%)
  matrix products  4.11 us (2%)
    pallas_call x2, Pallas kernels, attend_part(): pl.pallas_call(attend_kernel, grid=(length // KV_BLOCK,), in_specs=[whole...  120 us
    all_gather x1, waiting for transfers between devices, per_device(): lax.all_gather(gathered[:half], 'cols', axis=0, tiled=True)  26.9 us
    ppermute x7, starting transfers between devices, gather_rows(): pieces.append(lax.ppermute(value, axis, pairs))  12.1 us
    convert_element_type x1, other arithmetic, per_device(): jax.nn.gelu(spread, approximate=False).astype(jnp.bfloat16)  9 us
    ppermute x7, waiting for transfers between devices, gather_rows(): pieces.append(lax.ppermute(value, axis, pairs))  8.2 us
    ppermute x2, starting transfers between devices, padded_2(): after = lax.ppermute(initial, axis, down)  7.86 us
    ppermute x2, starting transfers between devices, padded_2(): before = lax.ppermute(last, axis, up)  7.43 us
  transfers between devices with their start and end apart: 13, of which 8 were waited for; matrix products, arithmetic and copies ran while one was open for 4% of the time, Pallas kernels for 25%

profile of v4, /device:TPU:15, one launch (start us, length us, event | category | flops | bytes accessed | tf_op | source)
XLA Modules:
  0.0 236.5 jit_solution(18240864844857789662)
XLA Ops:
  6.5 1.2 convert_reduce_fusion
  7.8 1.3 multiply_reduce_fusion
  9.1 0.1 reshape.177
  9.2 1.4 reshape.176
  10.7 0.1 reshape.178
  10.8 0.3 copy.74
  11.0 0.3 copy.71
  11.3 0.2 fusion.26
  11.6 0.3 copy.75
  11.9 0.3 reshape.166
  12.2 0.5 fusion.35
  12.7 0.2 multiply_reduce_fusion.2
  13.0 0.1 add_convert_fusion.4
  13.1 2.1 collective-permute-start.4
  15.2 0.2 collective-permute-start.5
  15.4 2.8 %collective-permute-start.6 = (bf16[128,320]{1,0:T(8,128)(2,1)S(1)}, bf16[128,320]{1,0:T(8,128)(2,1)S(1)}, u32[]{:S(2)}, u32[]{:S(2)}) collective-permute-start(bf16[128,320]{1,0:T(8,128)(2,1)S(1)} %add_convert_fusion.4), channel_id=1, source_target_pairs={{0,48},{16,64},{32,80},{48,96},{64,112},{80,0},{96,16},{112,32},{1... | collective-permute-start | bytes 245768 | tf_op jit(solution)/shard_map/ppermute | solution.py:29
  18.2 0.9 collective-permute-done.4
  19.0 3.7 %collective-permute-done.6 = bf16[128,320]{1,0:T(8,128)(2,1)S(1)} collective-permute-done((bf16[128,320]{1,0:T(8,128)(2,1)S(1)}, bf16[128,320]{1,0:T(8,128)(2,1)S(1)}, u32[]{:S(2)}, u32[]{:S(2)}) %collective-permute-start.6) | collective-permute-done | bytes 81952 | tf_op jit(solution)/shard_map/ppermute | solution.py:29
  22.8 0.8 pad_maximum_fusion.4
  23.6 2.2 collective-permute-start
  25.9 1.9 collective-permute-start.1
  27.8 0.6 collective-permute-start.2
  28.4 2.3 collective-permute-start.3
  30.7 2.4 collective-permute-done.1
  33.0 1.3 collective-permute-done.3
  34.3 0.8 pad_maximum_fusion.3
  35.1 0.1 rsqrt.32
  35.2 0.1 div.33
  35.3 0.2 copy.82
  35.6 1.6 fusion.16
  37.2 0.3 copy.69
  37.5 0.2 copy.77
  37.7 0.2 copy.78
  38.0 0.2 copy.79
  38.2 0.2 copy.80
  38.5 0.7 compare_reduce_fusion
  39.9 0.3 scatter.4
  40.2 0.6 reshape.170.b_ref
  40.8 1.0 pad.18.q_ref
  41.7 1.1 fusion.20.w_ref
  42.8 26.9 %all-gather.5.cloned.1.call-done.rn_ref = bf16[8192,320]{1,0:T(8,128)(2,1)} async-done(((bf16[512,320]{1,0:T(8,128)(2,1)}), bf16[8192,320]{1,0:T(8,128)(2,1)}) %all-gather.5.cloned.1.call-update) | async-done | bytes 5242896 | tf_op jit(solution)/shard_map/all_gather | solution.py:171
  69.7 1.2 broadcast_in_dim.4.m_in_ref
  70.8 1.2 broadcast_in_dim.5.acc_in_ref
  72.0 60.0 %shard_map.208 = (f32[5,512,1]{2,1,0:T(8,128)}, f32[5,512,128]{2,1,0:T(8,128)}) custom-call(bf16[5,512,128]{2,1,0:T(8,128)(2,1)} %pad.18.q_ref, bf16[8192,320]{1,0:T(8,128)(2,1)} %all-gather.5.cloned.1.call-done.rn_ref, bf16[5,320,256]{2,1,0:T(8,128)(2,1)} %fusion.20.w_ref, f32[5,1,256]{2,1,0:T(1,128)} %reshape.170.b_ref, ...), custom_call_target="tpu_custom_call" | custom-call | tf_op jit(solution)/shard_map/pallas_call | solution.py:80
  132.0 60.1 %shard_map.209 = (f32[5,512,1]{2,1,0:T(8,128)}, f32[5,512,128]{2,1,0:T(8,128)}) custom-call(bf16[5,512,128]{2,1,0:T(8,128)(2,1)} %pad.18.q_ref, bf16[8192,320]{1,0:T(8,128)(2,1)} %all-gather.3.cloned.1.call-done.rn_ref, bf16[5,320,256]{2,1,0:T(8,128)(2,1)} %fusion.20.w_ref, f32[5,1,256]{2,1,0:T(1,128)} %reshape.170.b_ref, ...), custom_call_target="tpu_custom_call" | custom-call | tf_op jit(solution)/shard_map/pallas_call | solution.py:80
  192.1 2.1 slice_reduce_fusion
  194.2 1.7 fusion.25
  196.0 0.2 copy.81
  196.2 0.4 fusion.36
  196.6 0.1 multiply_reduce_fusion.1
  196.8 1.0 fusion
  197.8 3.5 %collective-permute-start.7 = (bf16[1,16,1280]{2,1,0:T(8,128)(2,1)S(1)}, bf16[1,16,1280]{2,1,0:T(8,128)(2,1)S(1)}, u32[]{:S(2)}, u32[]{:S(2)}) collective-permute-start(bf16[1,16,1280]{2,1,0:T(8,128)(2,1)S(1)} %get-tuple-element.36), channel_id=1, source_target_pairs={{0,16},{16,32},{32,48},{48,64},{64,80},{80,96},{96,112},{1,17},{17... | collective-permute-start | bytes 122888 | tf_op jit(solution)/shard_map/ppermute | solution.py:18
  201.3 4.2 %collective-permute-start.8 = (bf16[1,16,1280]{2,1,0:T(8,128)(2,1)S(1)}, bf16[1,16,1280]{2,1,0:T(8,128)(2,1)S(1)}, u32[]{:S(2)}, u32[]{:S(2)}) collective-permute-start(bf16[1,16,1280]{2,1,0:T(8,128)(2,1)S(1)} %get-tuple-element.37), channel_id=1, source_target_pairs={{16,0},{32,16},{48,32},{64,48},{80,64},{96,80},{112,96},{17,1},{33... | collective-permute-start | bytes 122888 | tf_op jit(solution)/shard_map/ppermute | solution.py:19
  205.6 2.0 collective-permute-done.8
  207.6 0.3 pad_maximum_fusion.7
  207.8 3.6 %collective-permute-start.10 = (bf16[34,1,1280]{2,1,0:T(2,128)(2,1)S(1)}, bf16[34,1,1280]{2,1,0:T(2,128)(2,1)S(1)}, u32[]{:S(2)}, u32[]{:S(2)}) collective-permute-start(bf16[34,1,1280]{2,1,0:T(2,128)(2,1)S(1)} %get-tuple-element.35), channel_id=1, source_target_pairs={{1,0},{2,1},{3,2},{4,3},{5,4},{6,5},{7,6},{8,7},{9,8},{10,9},{11,1... | collective-permute-start | bytes 261128 | tf_op jit(solution)/shard_map/ppermute | solution.py:19
  211.5 4.0 %collective-permute-start.9 = (bf16[34,1,1280]{2,1,0:T(2,128)(2,1)S(1)}, bf16[34,1,1280]{2,1,0:T(2,128)(2,1)S(1)}, u32[]{:S(2)}, u32[]{:S(2)}) collective-permute-start(bf16[34,1,1280]{2,1,0:T(2,128)(2,1)S(1)} %get-tuple-element.34), channel_id=1, source_target_pairs={{0,1},{1,2},{2,3},{3,4},{4,5},{5,6},{6,7},{7,8},{8,9},{9,10},{10,1... | collective-permute-start | bytes 261128 | tf_op jit(solution)/shard_map/ppermute | solution.py:18
  215.5 0.1 slice_reduce_fusion.9
  215.6 1.0 collective-permute-done.10
  216.6 1.2 collective-permute-done.9
  217.8 1.3 maximum_maximum_fusion
  219.1 9.0 %fusion.3 = bf16[32,16,1280]{2,1,0:T(8,128)(2,1)S(1)} fusion(bf16[32,16,1280]{2,1,0:T(8,128)(2,1)S(1)} %bitcast.29, bf16[34,17,1280]{2,1,0:T(8,128)(2,1)S(1)} %get-tuple-element.33, bf16[1,16,1280]{2,1,0:T(8,128)(2,1)S(1)} %collective-permute-done.8, bf16[34,17,1280]{2,1,0:T(8,128)(2,1)S(1)} %get-tuple-element.32, ...), kind=kLoop, calls=%fused_computation.5 | loop fusion | flops 61603840 | bytes 10618880 | tf_op jit(solution)/shard_map/convert_element_type | solution.py:192
  228.1 0.6 fusion.19
  228.7 0.9 copy.83
  (63 shorter events, 0.4 us)
Async XLA Ops:
  6.5 190.2 %copy-start = (bf16[320,1280]{1,0:T(8,128)(2,1)S(1)}, bf16[320,1280]{1,0:T(8,128)(2,1)}, u32[]{:S(2)}) copy-start(bf16[320,1280]{1,0:T(8,128)(2,1)} %param.40) | copy-start | bytes 2457604
  6.5 4.8 %copy-start.12 = (f32[320]{0:T(512)S(1)}, f32[320]{0:T(512)}, u32[]{:S(2)}) copy-start(f32[320]{0:T(512)} %param.25) | copy-start | bytes 3844
  6.5 4.8 %copy-start.11 = (f32[320]{0:T(512)S(1)}, f32[320]{0:T(512)}, u32[]{:S(2)}) copy-start(f32[320]{0:T(512)} %param.26) | copy-start | bytes 3844
  6.5 63.1 %all-gather.5.cloned.1.call-start = ((), (), s32[]{:S(2)}) async-start(), calls=%async_computation.1 | async-start | bytes 6684672 | tf_op jit(solution)/shard_map/all_gather | solution.py:171
  7.8 4.4 %copy-start.2 = (bf16[1280,320]{0,1:T(8,128)(2,1)S(1)}, bf16[1280,320]{0,1:T(8,128)(2,1)}, u32[]{:S(2)}) copy-start(bf16[1280,320]{0,1:T(8,128)(2,1)} %param.29) | copy-start | bytes 2457604
  7.8 4.4 %copy-start.8 = (f32[320]{0:T(512)S(1)}, f32[320]{0:T(512)}, u32[]{:S(2)}) copy-start(f32[320]{0:T(512)} %param.30) | copy-start | bytes 3844
  10.6 2.3 copy-start.9
  10.7 2.3 copy-start.10
  11.9 23.4 %copy-start.1 = (bf16[32,16,320]{2,1,0:T(8,128)(2,1)S(1)}, bf16[32,16,320]{2,1,0:T(8,128)(2,1)}, u32[]{:S(2)}) copy-start(bf16[32,16,320]{2,1,0:T(8,128)(2,1)} %param.24) | copy-start | bytes 983044
  13.0 22.6 %copy-start.17 = (f32[320]{0:T(512)S(1)}, f32[320]{0:T(512)}, u32[]{:S(2)}) copy-start(f32[320]{0:T(512)} %param.28) | copy-start | bytes 3844
  13.1 5.9 %collective-permute-start.4 = (bf16[128,320]{1,0:T(8,128)(2,1)S(1)}, bf16[128,320]{1,0:T(8,128)(2,1)S(1)}, u32[]{:S(2)}, u32[]{:S(2)}) collective-permute-start(bf16[128,320]{1,0:T(8,128)(2,1)S(1)} %add_convert_fusion.4), channel_id=1, source_target_pairs={{0,16},{16,32},{32,48},{48,64},{64,80},{80,96},{96,112},{112,0},{1... | collective-permute-start | bytes 245768 | tf_op jit(solution)/shard_map/ppermute | solution.py:29
  15.2 3.9 %collective-permute-start.5 = (bf16[128,320]{1,0:T(8,128)(2,1)S(1)}, bf16[128,320]{1,0:T(8,128)(2,1)S(1)}, u32[]{:S(2)}, u32[]{:S(2)}) collective-permute-start(bf16[128,320]{1,0:T(8,128)(2,1)S(1)} %add_convert_fusion.4), channel_id=1, source_target_pairs={{0,32},{16,48},{32,64},{48,80},{64,96},{80,112},{96,0},{112,16},{1... | collective-permute-start | bytes 245768 | tf_op jit(solution)/shard_map/ppermute | solution.py:29
  15.4 7.4 %collective-permute-start.6 = (bf16[128,320]{1,0:T(8,128)(2,1)S(1)}, bf16[128,320]{1,0:T(8,128)(2,1)S(1)}, u32[]{:S(2)}, u32[]{:S(2)}) collective-permute-start(bf16[128,320]{1,0:T(8,128)(2,1)S(1)} %add_convert_fusion.4), channel_id=1, source_target_pairs={{0,48},{16,64},{32,80},{48,96},{64,112},{80,0},{96,16},{112,32},{1... | collective-permute-start | bytes 245768 | tf_op jit(solution)/shard_map/ppermute | solution.py:29
  23.6 108.4 %all-gather.3.cloned.1.call-start = ((), (), s32[]{:S(2)}) async-start(), calls=%async_computation | async-start | bytes 6684672 | tf_op jit(solution)/shard_map/all_gather | solution.py:172
  23.6 7.0 %collective-permute-start = (bf16[128,320]{1,0:T(8,128)(2,1)S(1)}, bf16[128,320]{1,0:T(8,128)(2,1)S(1)}, u32[]{:S(2)}, u32[]{:S(2)}) collective-permute-start(bf16[128,320]{1,0:T(8,128)(2,1)S(1)} %add_convert_fusion.4), channel_id=1, source_target_pairs={{0,64},{16,80},{32,96},{48,112},{64,0},{80,16},{96,32},{112,48},{1... | collective-permute-start | bytes 245768 | tf_op jit(solution)/shard_map/ppermute | solution.py:29
  25.9 7.1 %collective-permute-start.1 = (bf16[128,320]{1,0:T(8,128)(2,1)S(1)}, bf16[128,320]{1,0:T(8,128)(2,1)S(1)}, u32[]{:S(2)}, u32[]{:S(2)}) collective-permute-start(bf16[128,320]{1,0:T(8,128)(2,1)S(1)} %add_convert_fusion.4), channel_id=1, source_target_pairs={{0,80},{16,96},{32,112},{48,0},{64,16},{80,32},{96,48},{112,64},{1... | collective-permute-start | bytes 245768 | tf_op jit(solution)/shard_map/ppermute | solution.py:29
  27.8 5.2 %collective-permute-start.2 = (bf16[128,320]{1,0:T(8,128)(2,1)S(1)}, bf16[128,320]{1,0:T(8,128)(2,1)S(1)}, u32[]{:S(2)}, u32[]{:S(2)}) collective-permute-start(bf16[128,320]{1,0:T(8,128)(2,1)S(1)} %add_convert_fusion.4), channel_id=1, source_target_pairs={{0,96},{16,112},{32,0},{48,16},{64,32},{80,48},{96,64},{112,80},{1... | collective-permute-start | bytes 245768 | tf_op jit(solution)/shard_map/ppermute | solution.py:29
  28.4 5.9 %collective-permute-start.3 = (bf16[128,320]{1,0:T(8,128)(2,1)S(1)}, bf16[128,320]{1,0:T(8,128)(2,1)S(1)}, u32[]{:S(2)}, u32[]{:S(2)}) collective-permute-start(bf16[128,320]{1,0:T(8,128)(2,1)S(1)} %add_convert_fusion.4), channel_id=1, source_target_pairs={{0,112},{16,0},{32,16},{48,32},{64,48},{80,64},{96,80},{112,96},{1... | collective-permute-start | bytes 245768 | tf_op jit(solution)/shard_map/ppermute | solution.py:29
  35.3 2.3 copy-start.4
  35.3 2.6 %copy-start.5 = (bf16[320,320]{1,0:T(8,128)(2,1)S(1)}, bf16[320,320]{1,0:T(8,128)(2,1)}, u32[]{:S(2)}) copy-start(bf16[320,320]{1,0:T(8,128)(2,1)} %param.34) | copy-start | bytes 614404
  37.2 1.2 copy-start.14
  192.1 4.2 %copy-start.3 = (bf16[320,320]{1,0:T(8,128)(2,1)S(1)}, bf16[320,320]{1,0:T(8,128)(2,1)}, u32[]{:S(2)}) copy-start(bf16[320,320]{1,0:T(8,128)(2,1)} %param.36) | copy-start | bytes 614404
  192.1 4.2 %copy-start.13 = (f32[320]{0:T(512)S(1)}, f32[320]{0:T(512)}, u32[]{:S(2)}) copy-start(f32[320]{0:T(512)} %param.37) | copy-start | bytes 3844
  194.2 2.6 %copy-start.16 = (f32[1280]{0:T(1024)S(1)}, f32[1280]{0:T(1024)}, u32[]{:S(2)}) copy-start(f32[1280]{0:T(1024)} %param.41) | copy-start | bytes 15364
  194.2 2.6 %copy-start.18 = (f32[320]{0:T(512)S(1)}, f32[320]{0:T(512)}, u32[]{:S(2)}) copy-start(f32[320]{0:T(512)} %param.39) | copy-start | bytes 3844
  194.2 2.6 %copy-start.19 = (f32[320]{0:T(512)S(1)}, f32[320]{0:T(512)}, u32[]{:S(2)}) copy-start(f32[320]{0:T(512)} %param.38) | copy-start | bytes 3844
  196.8 18.7 %copy-start.6 = (f32[9,1280]{1,0:T(8,128)S(1)}, f32[9,1280]{1,0:T(8,128)}, u32[]{:S(2)}) copy-start(f32[9,1280]{1,0:T(8,128)} %param.42) | copy-start | bytes 138244
  197.8 7.7 %collective-permute-start.7 = (bf16[1,16,1280]{2,1,0:T(8,128)(2,1)S(1)}, bf16[1,16,1280]{2,1,0:T(8,128)(2,1)S(1)}, u32[]{:S(2)}, u32[]{:S(2)}) collective-permute-start(bf16[1,16,1280]{2,1,0:T(8,128)(2,1)S(1)} %get-tuple-element.36), channel_id=1, source_target_pairs={{0,16},{16,32},{32,48},{48,64},{64,80},{80,96},{96,112},{1,17},{17... | collective-permute-start | bytes 122888 | tf_op jit(solution)/shard_map/ppermute | solution.py:18
  201.3 6.3 %collective-permute-start.8 = (bf16[1,16,1280]{2,1,0:T(8,128)(2,1)S(1)}, bf16[1,16,1280]{2,1,0:T(8,128)(2,1)S(1)}, u32[]{:S(2)}, u32[]{:S(2)}) collective-permute-start(bf16[1,16,1280]{2,1,0:T(8,128)(2,1)S(1)} %get-tuple-element.37), channel_id=1, source_target_pairs={{16,0},{32,16},{48,32},{64,48},{80,64},{96,80},{112,96},{17,1},{33... | collective-permute-start | bytes 122888 | tf_op jit(solution)/shard_map/ppermute | solution.py:19
  207.8 8.8 %collective-permute-start.10 = (bf16[34,1,1280]{2,1,0:T(2,128)(2,1)S(1)}, bf16[34,1,1280]{2,1,0:T(2,128)(2,1)S(1)}, u32[]{:S(2)}, u32[]{:S(2)}) collective-permute-start(bf16[34,1,1280]{2,1,0:T(2,128)(2,1)S(1)} %get-tuple-element.35), channel_id=1, source_target_pairs={{1,0},{2,1},{3,2},{4,3},{5,4},{6,5},{7,6},{8,7},{9,8},{10,9},{11,1... | collective-permute-start | bytes 261128 | tf_op jit(solution)/shard_map/ppermute | solution.py:19
  211.5 6.3 %collective-permute-start.9 = (bf16[34,1,1280]{2,1,0:T(2,128)(2,1)S(1)}, bf16[34,1,1280]{2,1,0:T(2,128)(2,1)S(1)}, u32[]{:S(2)}, u32[]{:S(2)}) collective-permute-start(bf16[34,1,1280]{2,1,0:T(2,128)(2,1)S(1)} %get-tuple-element.34), channel_id=1, source_target_pairs={{0,1},{1,2},{2,3},{3,4},{4,5},{5,6},{6,7},{7,8},{8,9},{9,10},{10,1... | collective-permute-start | bytes 261128 | tf_op jit(solution)/shard_map/ppermute | solution.py:18
  215.6 3.5 %copy-start.7 = (f32[1280]{0:T(1024)S(1)}, f32[1280]{0:T(1024)}, u32[]{:S(2)}) copy-start(f32[1280]{0:T(1024)} %param.43) | copy-start | bytes 15364
  219.1 9.0 %copy-start.15 = (bf16[1280,320]{0,1:T(8,128)(2,1)S(1)}, bf16[1280,320]{0,1:T(8,128)(2,1)}, u32[]{:S(2)}) copy-start(bf16[1280,320]{0,1:T(8,128)(2,1)} %param.44) | copy-start | bytes 2457604
  219.1 9.0 %copy-start.20 = (f32[320]{0:T(512)S(1)}, f32[320]{0:T(512)}, u32[]{:S(2)}) copy-start(f32[320]{0:T(512)} %param.45) | copy-start | bytes 3844
Sparse Core Ops, SparseCore 0:
  23.7 45.9 all-gather.4
  71.4 42.9 all-gather.2

commit v5 on v4

--- a/solution.py
+++ b/solution.py
@@ -8,17 +8,30 @@
 HEADS = 5
 
 
-def padded_2(value, sides, width):
-    for axis, dim in sides:
-        devices, length = (lax.axis_size(axis), value.shape[dim])
-        up = [(i, (i + 1) % devices) for i in range(devices - 1)]
-        down = [(j, i) for i, j in up]
-        last = lax.slice_in_dim(value, length - width, length, axis=dim)
-        initial = lax.slice_in_dim(value, 0, width, axis=dim)
-        before = lax.ppermute(last, axis, up)
-        after = lax.ppermute(initial, axis, down)
-        value = jnp.concatenate([before, value, after], axis=dim)
-    return value
+def halo(value):
+    rows, cols = lax.axis_size("rows"), lax.axis_size("cols")
+    grid = [(r, c) for r in range(rows) for c in range(cols)]
+
+    def shifted(piece, dr, dc):
+        pairs = [
+            (r * cols + c, (r + dr) * cols + c + dc)
+            for r, c in grid
+            if 0 <= r + dr < rows and 0 <= c + dc < cols
+        ]
+        return lax.ppermute(piece, ("rows", "cols"), pairs)
+
+    top = shifted(value[-1:], 1, 0)
+    bottom = shifted(value[:1], -1, 0)
+    left = shifted(value[:, -1:], 0, 1)
+    right = shifted(value[:, :1], 0, -1)
+    top_left = shifted(value[-1:, -1:], 1, 1)
+    top_right = shifted(value[-1:, :1], 1, -1)
+    bottom_left = shifted(value[:1, -1:], -1, 1)
+    bottom_right = shifted(value[:1, :1], -1, -1)
+    upper = jnp.concatenate([top_left, top, top_right], axis=1)
+    middle = jnp.concatenate([left, value, right], axis=1)
+    lower = jnp.concatenate([bottom_left, bottom, bottom_right], axis=1)
+    return jnp.concatenate([upper, middle, lower], axis=0)
 
 
 def gather_rows(value, axis):
@@ -180,7 +193,7 @@
     expanded = (jnp.dot(normed2, w_expand, preferred_element_type=jnp.float32) + b_expand).astype(
         jnp.bfloat16
     )
-    padded = padded_2(expanded.reshape(tile_r, tile_c, ffn), (("rows", 0), ("cols", 1)), 1)
+    padded = halo(expanded.reshape(tile_r, tile_c, ffn))
     spread = jnp.zeros((tile_r, tile_c, ffn), jnp.float32) + b_depth
     for tap_r in range(3):
         for tap_c in range(3):

time: 238 us -> 254 us (1.067)
  starting transfers between devices: 27.4 us -> 37.9 us
  other arithmetic: 18.9 us -> 22.5 us
    ppermute x4 -> x8, starting transfers between devices: 15.3 us -> 25.8 us  [shifted(): return lax.ppermute(piece, ('rows', 'cols'), pairs)]
    concatenate x1, other arithmetic: 1.25 us -> 4.69 us  [halo(): return jnp.concatenate([upper, middle, lower], axis=0)]
    ppermute x4 -> x8, waiting for transfers between devices: 4.2 us -> 5.36 us  [shifted(): return lax.ppermute(piece, ('rows', 'cols'), pairs)]
  transfers between devices with their start and end apart: 13 -> 17, of which waited for: 8 -> 6; matrix products, arithmetic and copies ran while one was open for 4% -> 4% of each run, Pallas kernels for 25% -> 24%
where the time goes in v5:
time: 254 us; the launch traced here: 252 us
  Pallas kernels  120 us (47%)
  waiting for transfers between devices  40.6 us (16%)
  starting transfers between devices  37.9 us (15%)
  other arithmetic  22.5 us (9%)
  between operations  14.6 us (6%)
  local copies, waits for them, and re-layouts  12.3 us (5%)
  matrix products  4.09 us (2%)
    pallas_call x2, Pallas kernels, attend_part(): pl.pallas_call(attend_kernel, grid=(length // KV_BLOCK,), in_specs=[whole...  120 us
    all_gather x1, waiting for transfers between devices, per_device(): lax.all_gather(gathered[:half], 'cols', axis=0, tiled=True)  27 us
    ppermute x8, starting transfers between devices, shifted(): return lax.ppermute(piece, ('rows', 'cols'), pairs)  25.8 us
    ppermute x7, starting transfers between devices, gather_rows(): pieces.append(lax.ppermute(value, axis, pairs))  12.1 us
    convert_element_type x1, other arithmetic, per_device(): jax.nn.gelu(spread, approximate=False).astype(jnp.bfloat16)  9.48 us
    ppermute x7, waiting for transfers between devices, gather_rows(): pieces.append(lax.ppermute(value, axis, pairs))  8.2 us
    ppermute x8, waiting for transfers between devices, shifted(): return lax.ppermute(piece, ('rows', 'cols'), pairs)  5.36 us
  transfers between devices with their start and end apart: 17, of which 6 were waited for; matrix products, arithmetic and copies ran while one was open for 4% of the time, Pallas kernels for 24%

profile of v5, /device:TPU:15, one launch (start us, length us, event | category | flops | bytes accessed | tf_op | source)
XLA Modules:
  0.0 252.1 jit_solution(10021764836224945714)
XLA Ops:
  6.5 1.2 convert_reduce_fusion
  7.8 1.3 multiply_reduce_fusion
  9.1 0.1 reshape.177
  9.2 1.4 reshape.176
  10.7 0.1 reshape.178
  10.8 0.3 copy.74
  11.0 0.3 copy.71
  11.3 0.2 fusion.26
  11.6 0.3 copy.75
  11.9 0.3 reshape.166
  12.2 0.5 fusion.37
  12.7 0.2 multiply_reduce_fusion.2
  13.0 0.1 add_convert_fusion.4
  13.1 2.1 collective-permute-start.4
  15.2 0.2 collective-permute-start.5
  15.4 2.8 %collective-permute-start.6 = (bf16[128,320]{1,0:T(8,128)(2,1)S(1)}, bf16[128,320]{1,0:T(8,128)(2,1)S(1)}, u32[]{:S(2)}, u32[]{:S(2)}) collective-permute-start(bf16[128,320]{1,0:T(8,128)(2,1)S(1)} %add_convert_fusion.4), channel_id=1, source_target_pairs={{0,48},{16,64},{32,80},{48,96},{64,112},{80,0},{96,16},{112,32},{1... | collective-permute-start | bytes 245768 | tf_op jit(solution)/shard_map/ppermute | solution.py:42
  18.2 0.9 collective-permute-done.4
  19.0 3.7 %collective-permute-done.6 = bf16[128,320]{1,0:T(8,128)(2,1)S(1)} collective-permute-done((bf16[128,320]{1,0:T(8,128)(2,1)S(1)}, bf16[128,320]{1,0:T(8,128)(2,1)S(1)}, u32[]{:S(2)}, u32[]{:S(2)}) %collective-permute-start.6) | collective-permute-done | bytes 81952 | tf_op jit(solution)/shard_map/ppermute | solution.py:42
  22.8 0.8 pad_maximum_fusion.3
  23.6 2.2 collective-permute-start
  25.8 1.9 collective-permute-start.1
  27.8 0.6 collective-permute-start.2
  28.4 2.3 collective-permute-start.3
  30.6 2.4 collective-permute-done.1
  33.0 1.3 collective-permute-done.3
  34.3 0.8 pad_maximum_fusion.2
  35.3 0.2 copy.82
  35.6 1.6 fusion.16
  37.2 0.3 copy.69
  37.5 0.2 copy.77
  37.7 0.2 copy.78
  38.0 0.2 copy.79
  38.2 0.2 copy.80
  38.5 0.7 compare_reduce_fusion
  39.8 0.3 scatter.4
  40.1 0.6 reshape.170.b_ref
  40.6 1.0 pad.18.q_ref
  41.6 1.1 fusion.20.w_ref
  42.7 27.0 %all-gather.5.cloned.1.call-done.rn_ref = bf16[8192,320]{1,0:T(8,128)(2,1)} async-done(((bf16[512,320]{1,0:T(8,128)(2,1)}), bf16[8192,320]{1,0:T(8,128)(2,1)}) %all-gather.5.cloned.1.call-update) | async-done | bytes 5242896 | tf_op jit(solution)/shard_map/all_gather | solution.py:184
  69.7 1.2 broadcast_in_dim.4.m_in_ref
  70.8 1.2 broadcast_in_dim.5.acc_in_ref
  72.0 60.0 %shard_map.208 = (f32[5,512,1]{2,1,0:T(8,128)}, f32[5,512,128]{2,1,0:T(8,128)}) custom-call(bf16[5,512,128]{2,1,0:T(8,128)(2,1)} %pad.18.q_ref, bf16[8192,320]{1,0:T(8,128)(2,1)} %all-gather.5.cloned.1.call-done.rn_ref, bf16[5,320,256]{2,1,0:T(8,128)(2,1)} %fusion.20.w_ref, f32[5,1,256]{2,1,0:T(1,128)} %reshape.170.b_ref, ...), custom_call_target="tpu_custom_call" | custom-call | tf_op jit(solution)/shard_map/pallas_call | solution.py:93
  132.0 60.1 %shard_map.209 = (f32[5,512,1]{2,1,0:T(8,128)}, f32[5,512,128]{2,1,0:T(8,128)}) custom-call(bf16[5,512,128]{2,1,0:T(8,128)(2,1)} %pad.18.q_ref, bf16[8192,320]{1,0:T(8,128)(2,1)} %all-gather.3.cloned.1.call-done.rn_ref, bf16[5,320,256]{2,1,0:T(8,128)(2,1)} %fusion.20.w_ref, f32[5,1,256]{2,1,0:T(1,128)} %reshape.170.b_ref, ...), custom_call_target="tpu_custom_call" | custom-call | tf_op jit(solution)/shard_map/pallas_call | solution.py:93
  192.0 2.1 slice_reduce_fusion
  194.2 1.7 fusion.25
  195.9 0.2 copy.81
  196.2 0.4 fusion.38
  196.6 0.1 multiply_reduce_fusion.1
  196.8 1.0 fusion
  197.8 0.3 fusion.36
  198.1 4.3 %collective-permute-start.12 = (bf16[1,1,1280]{2,1,0:T(2,128)(2,1)S(1)}, bf16[1,1,1280]{2,1,0:T(2,128)(2,1)S(1)}, u32[]{:S(2)}, u32[]{:S(2)}) collective-permute-start(bf16[1,1,1280]{2,1,0:T(2,128)(2,1)S(1)} %get-tuple-element.35), channel_id=1, source_target_pairs={{16,1},{17,2},{18,3},{19,4},{20,5},{21,6},{22,7},{23,8},{24,9},{25... | collective-permute-start | bytes 7688 | tf_op jit(solution)/shard_map/ppermute | solution.py:21
  202.4 3.4 %collective-permute-start.14 = (bf16[1,1,1280]{2,1,0:T(2,128)(2,1)S(1)}, bf16[1,1,1280]{2,1,0:T(2,128)(2,1)S(1)}, u32[]{:S(2)}, u32[]{:S(2)}) collective-permute-start(bf16[1,1,1280]{2,1,0:T(2,128)(2,1)S(1)} %get-tuple-element.36), channel_id=1, source_target_pairs={{17,0},{18,1},{19,2},{20,3},{21,4},{22,5},{23,6},{24,7},{25,8},{26... | collective-permute-start | bytes 7688 | tf_op jit(solution)/shard_map/ppermute | solution.py:21
  205.8 3.0 %collective-permute-start.7 = (bf16[1,1,1280]{2,1,0:T(2,128)(2,1)S(1)}, bf16[1,1,1280]{2,1,0:T(2,128)(2,1)S(1)}, u32[]{:S(2)}, u32[]{:S(2)}) collective-permute-start(bf16[1,1,1280]{2,1,0:T(2,128)(2,1)S(1)} %get-tuple-element.34), channel_id=1, source_target_pairs={{0,17},{1,18},{2,19},{3,20},{4,21},{5,22},{6,23},{7,24},{8,25},{9,... | collective-permute-start | bytes 7688 | tf_op jit(solution)/shard_map/ppermute | solution.py:21
  208.9 4.4 %collective-permute-start.10 = (bf16[32,1,1280]{2,1,0:T(2,128)(2,1)S(1)}, bf16[32,1,1280]{2,1,0:T(2,128)(2,1)S(1)}, u32[]{:S(2)}, u32[]{:S(2)}) collective-permute-start(bf16[32,1,1280]{2,1,0:T(2,128)(2,1)S(1)} %get-tuple-element.40), channel_id=1, source_target_pairs={{0,1},{1,2},{2,3},{3,4},{4,5},{5,6},{6,7},{7,8},{8,9},{9,10},{10,1... | collective-permute-start | bytes 245768 | tf_op jit(solution)/shard_map/ppermute | solution.py:21
  213.3 1.9 collective-permute-start.11
  215.2 3.6 %collective-permute-start.13 = (bf16[1,16,1280]{2,1,0:T(8,128)(2,1)S(1)}, bf16[1,16,1280]{2,1,0:T(8,128)(2,1)S(1)}, u32[]{:S(2)}, u32[]{:S(2)}) collective-permute-start(bf16[1,16,1280]{2,1,0:T(8,128)(2,1)S(1)} %get-tuple-element.39), channel_id=1, source_target_pairs={{16,0},{17,1},{18,2},{19,3},{20,4},{21,5},{22,6},{23,7},{24,8},{25... | collective-permute-start | bytes 122888 | tf_op jit(solution)/shard_map/ppermute | solution.py:21
  218.9 3.2 %collective-permute-start.8 = (bf16[1,16,1280]{2,1,0:T(8,128)(2,1)S(1)}, bf16[1,16,1280]{2,1,0:T(8,128)(2,1)S(1)}, u32[]{:S(2)}, u32[]{:S(2)}) collective-permute-start(bf16[1,16,1280]{2,1,0:T(8,128)(2,1)S(1)} %get-tuple-element.38), channel_id=1, source_target_pairs={{0,16},{1,17},{2,18},{3,19},{4,20},{5,21},{6,22},{7,23},{8,24},{9,... | collective-permute-start | bytes 122888 | tf_op jit(solution)/shard_map/ppermute | solution.py:21
  222.1 1.9 collective-permute-start.9
  224.0 0.1 slice_reduce_fusion.9
  224.1 5.3 %collective-permute-done.9 = bf16[1,1,1280]{2,1,0:T(2,128)(2,1)S(1)} collective-permute-done((bf16[1,1,1280]{2,1,0:T(2,128)(2,1)S(1)}, bf16[1,1,1280]{2,1,0:T(2,128)(2,1)S(1)}, u32[]{:S(2)}, u32[]{:S(2)}) %collective-permute-start.9) | collective-permute-done | bytes 2592 | tf_op jit(solution)/shard_map/ppermute | solution.py:21
  229.5 4.7 %maximum_maximum_fusion = (bf16[33,18,1280]{2,1,0:T(8,128)(2,1)S(1)}, bf16[33,18,1280]{2,1,0:T(8,128)(2,1)S(1)}) fusion(bf16[32,1,1280]{2,1,0:T(2,128)(2,1)S(1)} %collective-permute-done.11, bf16[32,16,1280]{2,1,0:T(8,128)(2,1)S(1)} %bitcast.29, bf16[32,1,1280]{2,1,0:T(2,128)(2,1)S(1)} %collective-permute-done.10, ...), kind=kLoop, calls=%fused_computation.22 | loop fusion | flops 18247680 | bytes 4608000 | tf_op jit(solution)/shard_map/concatenate | solution.py:34
  234.2 9.5 %fusion.3 = bf16[32,16,1280]{2,1,0:T(8,128)(2,1)S(1)} fusion(bf16[32,16,1280]{2,1,0:T(8,128)(2,1)S(1)} %bitcast.30, bf16[33,18,1280]{2,1,0:T(8,128)(2,1)S(1)} %get-tuple-element.33, bf16[32,1,1280]{2,1,0:T(2,128)(2,1)S(1)} %collective-permute-done.11, bf16[32,1,1280]{2,1,0:T(2,128)(2,1)S(1)} %collective-permute-done.10, ...), kind=kLoop, calls=%fused_computation.5 | loop fusion | flops 64225280 | bytes 10700800 | tf_op jit(solution)/shard_map/convert_element_type | solution.py:205
  243.7 0.6 fusion.19
  244.4 0.9 copy.83
  (72 shorter events, 0.6 us)
Async XLA Ops:
  6.5 190.2 %copy-start = (bf16[320,1280]{1,0:T(8,128)(2,1)S(1)}, bf16[320,1280]{1,0:T(8,128)(2,1)}, u32[]{:S(2)}) copy-start(bf16[320,1280]{1,0:T(8,128)(2,1)} %param.40) | copy-start | bytes 2457604
  6.5 4.8 %copy-start.12 = (f32[320]{0:T(512)S(1)}, f32[320]{0:T(512)}, u32[]{:S(2)}) copy-start(f32[320]{0:T(512)} %param.25) | copy-start | bytes 3844
  6.5 4.8 %copy-start.11 = (f32[320]{0:T(512)S(1)}, f32[320]{0:T(512)}, u32[]{:S(2)}) copy-start(f32[320]{0:T(512)} %param.26) | copy-start | bytes 3844
  6.5 63.1 %all-gather.5.cloned.1.call-start = ((), (), s32[]{:S(2)}) async-start(), calls=%async_computation.1 | async-start | bytes 6684672 | tf_op jit(solution)/shard_map/all_gather | solution.py:184
  7.8 4.4 %copy-start.2 = (bf16[1280,320]{0,1:T(8,128)(2,1)S(1)}, bf16[1280,320]{0,1:T(8,128)(2,1)}, u32[]{:S(2)}) copy-start(bf16[1280,320]{0,1:T(8,128)(2,1)} %param.29) | copy-start | bytes 2457604
  7.8 4.4 %copy-start.8 = (f32[320]{0:T(512)S(1)}, f32[320]{0:T(512)}, u32[]{:S(2)}) copy-start(f32[320]{0:T(512)} %param.30) | copy-start | bytes 3844
  10.6 2.3 copy-start.9
  10.7 2.3 copy-start.10
  11.9 23.4 %copy-start.1 = (bf16[32,16,320]{2,1,0:T(8,128)(2,1)S(1)}, bf16[32,16,320]{2,1,0:T(8,128)(2,1)}, u32[]{:S(2)}) copy-start(bf16[32,16,320]{2,1,0:T(8,128)(2,1)} %param.24) | copy-start | bytes 983044
  13.0 22.6 %copy-start.17 = (f32[320]{0:T(512)S(1)}, f32[320]{0:T(512)}, u32[]{:S(2)}) copy-start(f32[320]{0:T(512)} %param.28) | copy-start | bytes 3844
  13.1 5.9 %collective-permute-start.4 = (bf16[128,320]{1,0:T(8,128)(2,1)S(1)}, bf16[128,320]{1,0:T(8,128)(2,1)S(1)}, u32[]{:S(2)}, u32[]{:S(2)}) collective-permute-start(bf16[128,320]{1,0:T(8,128)(2,1)S(1)} %add_convert_fusion.4), channel_id=1, source_target_pairs={{0,16},{16,32},{32,48},{48,64},{64,80},{80,96},{96,112},{112,0},{1... | collective-permute-start | bytes 245768 | tf_op jit(solution)/shard_map/ppermute | solution.py:42
  15.2 3.9 %collective-permute-start.5 = (bf16[128,320]{1,0:T(8,128)(2,1)S(1)}, bf16[128,320]{1,0:T(8,128)(2,1)S(1)}, u32[]{:S(2)}, u32[]{:S(2)}) collective-permute-start(bf16[128,320]{1,0:T(8,128)(2,1)S(1)} %add_convert_fusion.4), channel_id=1, source_target_pairs={{0,32},{16,48},{32,64},{48,80},{64,96},{80,112},{96,0},{112,16},{1... | collective-permute-start | bytes 245768 | tf_op jit(solution)/shard_map/ppermute | solution.py:42
  15.4 7.4 %collective-permute-start.6 = (bf16[128,320]{1,0:T(8,128)(2,1)S(1)}, bf16[128,320]{1,0:T(8,128)(2,1)S(1)}, u32[]{:S(2)}, u32[]{:S(2)}) collective-permute-start(bf16[128,320]{1,0:T(8,128)(2,1)S(1)} %add_convert_fusion.4), channel_id=1, source_target_pairs={{0,48},{16,64},{32,80},{48,96},{64,112},{80,0},{96,16},{112,32},{1... | collective-permute-start | bytes 245768 | tf_op jit(solution)/shard_map/ppermute | solution.py:42
  23.6 108.4 %all-gather.3.cloned.1.call-start = ((), (), s32[]{:S(2)}) async-start(), calls=%async_computation | async-start | bytes 6684672 | tf_op jit(solution)/shard_map/all_gather | solution.py:185
  23.6 7.0 %collective-permute-start = (bf16[128,320]{1,0:T(8,128)(2,1)S(1)}, bf16[128,320]{1,0:T(8,128)(2,1)S(1)}, u32[]{:S(2)}, u32[]{:S(2)}) collective-permute-start(bf16[128,320]{1,0:T(8,128)(2,1)S(1)} %add_convert_fusion.4), channel_id=1, source_target_pairs={{0,64},{16,80},{32,96},{48,112},{64,0},{80,16},{96,32},{112,48},{1... | collective-permute-start | bytes 245768 | tf_op jit(solution)/shard_map/ppermute | solution.py:42
  25.8 7.1 %collective-permute-start.1 = (bf16[128,320]{1,0:T(8,128)(2,1)S(1)}, bf16[128,320]{1,0:T(8,128)(2,1)S(1)}, u32[]{:S(2)}, u32[]{:S(2)}) collective-permute-start(bf16[128,320]{1,0:T(8,128)(2,1)S(1)} %add_convert_fusion.4), channel_id=1, source_target_pairs={{0,80},{16,96},{32,112},{48,0},{64,16},{80,32},{96,48},{112,64},{1... | collective-permute-start | bytes 245768 | tf_op jit(solution)/shard_map/ppermute | solution.py:42
  27.8 5.2 %collective-permute-start.2 = (bf16[128,320]{1,0:T(8,128)(2,1)S(1)}, bf16[128,320]{1,0:T(8,128)(2,1)S(1)}, u32[]{:S(2)}, u32[]{:S(2)}) collective-permute-start(bf16[128,320]{1,0:T(8,128)(2,1)S(1)} %add_convert_fusion.4), channel_id=1, source_target_pairs={{0,96},{16,112},{32,0},{48,16},{64,32},{80,48},{96,64},{112,80},{1... | collective-permute-start | bytes 245768 | tf_op jit(solution)/shard_map/ppermute | solution.py:42
  28.4 5.9 %collective-permute-start.3 = (bf16[128,320]{1,0:T(8,128)(2,1)S(1)}, bf16[128,320]{1,0:T(8,128)(2,1)S(1)}, u32[]{:S(2)}, u32[]{:S(2)}) collective-permute-start(bf16[128,320]{1,0:T(8,128)(2,1)S(1)} %add_convert_fusion.4), channel_id=1, source_target_pairs={{0,112},{16,0},{32,16},{48,32},{64,48},{80,64},{96,80},{112,96},{1... | collective-permute-start | bytes 245768 | tf_op jit(solution)/shard_map/ppermute | solution.py:42
  35.3 2.3 copy-start.4
  35.3 2.6 %copy-start.5 = (bf16[320,320]{1,0:T(8,128)(2,1)S(1)}, bf16[320,320]{1,0:T(8,128)(2,1)}, u32[]{:S(2)}) copy-start(bf16[320,320]{1,0:T(8,128)(2,1)} %param.34) | copy-start | bytes 614404
  37.2 1.2 copy-start.14
  192.0 4.2 %copy-start.3 = (bf16[320,320]{1,0:T(8,128)(2,1)S(1)}, bf16[320,320]{1,0:T(8,128)(2,1)}, u32[]{:S(2)}) copy-start(bf16[320,320]{1,0:T(8,128)(2,1)} %param.36) | copy-start | bytes 614404
  192.0 4.2 %copy-start.13 = (f32[320]{0:T(512)S(1)}, f32[320]{0:T(512)}, u32[]{:S(2)}) copy-start(f32[320]{0:T(512)} %param.37) | copy-start | bytes 3844
  194.2 2.6 %copy-start.16 = (f32[1280]{0:T(1024)S(1)}, f32[1280]{0:T(1024)}, u32[]{:S(2)}) copy-start(f32[1280]{0:T(1024)} %param.41) | copy-start | bytes 15364
  194.2 2.6 %copy-start.18 = (f32[320]{0:T(512)S(1)}, f32[320]{0:T(512)}, u32[]{:S(2)}) copy-start(f32[320]{0:T(512)} %param.39) | copy-start | bytes 3844
  194.2 2.6 %copy-start.19 = (f32[320]{0:T(512)S(1)}, f32[320]{0:T(512)}, u32[]{:S(2)}) copy-start(f32[320]{0:T(512)} %param.38) | copy-start | bytes 3844
  196.7 27.3 %copy-start.6 = (f32[9,1280]{1,0:T(8,128)S(1)}, f32[9,1280]{1,0:T(8,128)}, u32[]{:S(2)}) copy-start(f32[9,1280]{1,0:T(8,128)} %param.42) | copy-start | bytes 138244
  198.1 17.2 %collective-permute-start.12 = (bf16[1,1,1280]{2,1,0:T(2,128)(2,1)S(1)}, bf16[1,1,1280]{2,1,0:T(2,128)(2,1)S(1)}, u32[]{:S(2)}, u32[]{:S(2)}) collective-permute-start(bf16[1,1,1280]{2,1,0:T(2,128)(2,1)S(1)} %get-tuple-element.35), channel_id=1, source_target_pairs={{16,1},{17,2},{18,3},{19,4},{20,5},{21,6},{22,7},{23,8},{24,9},{25... | collective-permute-start | bytes 7688 | tf_op jit(solution)/shard_map/ppermute | solution.py:21
  202.4 16.5 %collective-permute-start.14 = (bf16[1,1,1280]{2,1,0:T(2,128)(2,1)S(1)}, bf16[1,1,1280]{2,1,0:T(2,128)(2,1)S(1)}, u32[]{:S(2)}, u32[]{:S(2)}) collective-permute-start(bf16[1,1,1280]{2,1,0:T(2,128)(2,1)S(1)} %get-tuple-element.36), channel_id=1, source_target_pairs={{17,0},{18,1},{19,2},{20,3},{21,4},{22,5},{23,6},{24,7},{25,8},{26... | collective-permute-start | bytes 7688 | tf_op jit(solution)/shard_map/ppermute | solution.py:21
  205.8 16.2 %collective-permute-start.7 = (bf16[1,1,1280]{2,1,0:T(2,128)(2,1)S(1)}, bf16[1,1,1280]{2,1,0:T(2,128)(2,1)S(1)}, u32[]{:S(2)}, u32[]{:S(2)}) collective-permute-start(bf16[1,1,1280]{2,1,0:T(2,128)(2,1)S(1)} %get-tuple-element.34), channel_id=1, source_target_pairs={{0,17},{1,18},{2,19},{3,20},{4,21},{5,22},{6,23},{7,24},{8,25},{9,... | collective-permute-start | bytes 7688 | tf_op jit(solution)/shard_map/ppermute | solution.py:21
  208.9 20.6 %collective-permute-start.10 = (bf16[32,1,1280]{2,1,0:T(2,128)(2,1)S(1)}, bf16[32,1,1280]{2,1,0:T(2,128)(2,1)S(1)}, u32[]{:S(2)}, u32[]{:S(2)}) collective-permute-start(bf16[32,1,1280]{2,1,0:T(2,128)(2,1)S(1)} %get-tuple-element.40), channel_id=1, source_target_pairs={{0,1},{1,2},{2,3},{3,4},{4,5},{5,6},{6,7},{7,8},{8,9},{9,10},{10,1... | collective-permute-start | bytes 245768 | tf_op jit(solution)/shard_map/ppermute | solution.py:21
  213.3 16.2 %collective-permute-start.11 = (bf16[32,1,1280]{2,1,0:T(2,128)(2,1)S(1)}, bf16[32,1,1280]{2,1,0:T(2,128)(2,1)S(1)}, u32[]{:S(2)}, u32[]{:S(2)}) collective-permute-start(bf16[32,1,1280]{2,1,0:T(2,128)(2,1)S(1)} %get-tuple-element.41), channel_id=1, source_target_pairs={{1,0},{2,1},{3,2},{4,3},{5,4},{6,5},{7,6},{8,7},{9,8},{10,9},{11,1... | collective-permute-start | bytes 245768 | tf_op jit(solution)/shard_map/ppermute | solution.py:21
  215.2 14.3 %collective-permute-start.13 = (bf16[1,16,1280]{2,1,0:T(8,128)(2,1)S(1)}, bf16[1,16,1280]{2,1,0:T(8,128)(2,1)S(1)}, u32[]{:S(2)}, u32[]{:S(2)}) collective-permute-start(bf16[1,16,1280]{2,1,0:T(8,128)(2,1)S(1)} %get-tuple-element.39), channel_id=1, source_target_pairs={{16,0},{17,1},{18,2},{19,3},{20,4},{21,5},{22,6},{23,7},{24,8},{25... | collective-permute-start | bytes 122888 | tf_op jit(solution)/shard_map/ppermute | solution.py:21
  218.9 10.6 %collective-permute-start.8 = (bf16[1,16,1280]{2,1,0:T(8,128)(2,1)S(1)}, bf16[1,16,1280]{2,1,0:T(8,128)(2,1)S(1)}, u32[]{:S(2)}, u32[]{:S(2)}) collective-permute-start(bf16[1,16,1280]{2,1,0:T(8,128)(2,1)S(1)} %get-tuple-element.38), channel_id=1, source_target_pairs={{0,16},{1,17},{2,18},{3,19},{4,20},{5,21},{6,22},{7,23},{8,24},{9,... | collective-permute-start | bytes 122888 | tf_op jit(solution)/shard_map/ppermute | solution.py:21
  222.1 7.4 %collective-permute-start.9 = (bf16[1,1,1280]{2,1,0:T(2,128)(2,1)S(1)}, bf16[1,1,1280]{2,1,0:T(2,128)(2,1)S(1)}, u32[]{:S(2)}, u32[]{:S(2)}) collective-permute-start(bf16[1,1,1280]{2,1,0:T(2,128)(2,1)S(1)} %get-tuple-element.37), channel_id=1, source_target_pairs={{1,16},{2,17},{3,18},{4,19},{5,20},{6,21},{7,22},{8,23},{9,24},{10... | collective-permute-start | bytes 7688 | tf_op jit(solution)/shard_map/ppermute | solution.py:21
  224.1 10.1 %copy-start.7 = (f32[1280]{0:T(1024)S(1)}, f32[1280]{0:T(1024)}, u32[]{:S(2)}) copy-start(f32[1280]{0:T(1024)} %param.43) | copy-start | bytes 15364
  234.2 9.5 %copy-start.15 = (bf16[1280,320]{0,1:T(8,128)(2,1)S(1)}, bf16[1280,320]{0,1:T(8,128)(2,1)}, u32[]{:S(2)}) copy-start(bf16[1280,320]{0,1:T(8,128)(2,1)} %param.44) | copy-start | bytes 2457604
  234.2 9.5 %copy-start.20 = (f32[320]{0:T(512)S(1)}, f32[320]{0:T(512)}, u32[]{:S(2)}) copy-start(f32[320]{0:T(512)} %param.45) | copy-start | bytes 3844
Sparse Core Ops, SparseCore 0:
  23.7 45.9 all-gather.4
  71.4 42.9 all-gather.2
